TPU v7x, 32 devices: a whole 2x2x4 slice. The times are simulated.
32 devices in a mesh: req: 4 (over z), ctx: 8 (over y, x, core).
Axes of the slice: x: 2, y: 2, z: 4, core: 2. Of those that a mesh axis runs over, the one named last changes fastest.
Arguments:
- hidden_in: bfloat16 [4096, 2048], P(('req', 'ctx')), may hold values from -3 to 3
- queries: bfloat16 [4096, 1024], P(('req', 'ctx')), may hold values from -10 to 10
- span_keys: bfloat16 [4096, 1024], P(('req', 'ctx')), may hold values from -10 to 10
- span_values: bfloat16 [4096, 1024], P(('req', 'ctx')), may hold values from -6 to 6
- cache_keys: bfloat16 [6144, 1024], P(('req', 'ctx')), may hold values from -6 to 6
- cache_values: bfloat16 [6144, 1024], P(('req', 'ctx')), may hold values from -6 to 6
- cache_lengths: int32 [4], replicated, may hold values from 0 to 1536, as said below
- slot_request: int32 [4], replicated, may hold values from 0 to 3, each once
- out_weight: bfloat16 [1024, 2048], replicated, may hold values from -1.5 to 1.5
- norm_gain: float32 [2048], replicated, may hold values from 0.1 to 1.9
- expert_ids: int32 [4096, 8], P(('req', 'ctx')), may hold values from 0 to 15, all different within a row; in each aligned block of 128 rows (0 to 127, 128 to 255, ...) at most 128 rows name the same one
- expert_gates: float32 [4096, 8], P(('req', 'ctx')), may hold values from 0.05 to 0.5
- gate_proj: bfloat16 [16, 2048, 512], P('ctx'), may hold values from -0.125 to 0.125
- up_proj: bfloat16 [16, 2048, 512], P('ctx'), may hold values from -0.125 to 0.125
- down_proj: bfloat16 [16, 512, 2048], P('ctx'), may hold values from -0.25 to 0.25
Outputs:
- layer_out: bfloat16 [4096, 2048], P(('req', 'ctx'))
Inputs may be any that keep to these rules, and one draw needn't show every extreme that they name: `cache_lengths`: some request has exactly 1536 cached positions.
All inputs are finite; a program needn't handle non-finite values.
Results may differ from a plain program's by a relative error of at most 0.015.
Values may be sent and summed in bfloat16 or wider, within the bound.
No kernel may reach another device: no remote copies, remote signals or barrier semaphores. Data moves between devices by JAX's collectives and lax.ppermute only.
A program may use at most 192 MiB of HBM per device.

v0:
```python
import itertools
import math

import jax
import jax.numpy as jnp
from jax import lax
from jax.experimental import pallas as pl
from jax.experimental.pallas import tpu as pltpu
from jax.sharding import PartitionSpec as P

HEAD_DIM = 128


def attend_gathered(queries, span_keys, span_values, cache_keys, cache_values, length):
    token_count, column_count = queries.shape
    head_count = column_count // HEAD_DIM
    cached_rows = cache_keys.shape[0]
    block_rows = token_count + cached_rows
    scaling = 1.0 / math.sqrt(HEAD_DIM)
    key_block = jnp.concatenate([span_keys, cache_keys], 0)
    value_block = jnp.concatenate([span_values, cache_values], 0)
    piece_keys = lax.all_gather(key_block, "ctx", axis=0, tiled=True)
    piece_values = lax.all_gather(value_block, "ctx", axis=0, tiled=True)
    piece_rows = piece_keys.shape[0]
    index = jnp.arange(piece_rows, dtype=jnp.int32)
    owner = index // block_rows
    within = index % block_rows
    usable = (within < token_count) | (owner * cached_rows + within - token_count < length)
    scores = (
        jnp.einsum(
            "thd,phd->htp",
            queries.reshape(token_count, head_count, HEAD_DIM),
            piece_keys.reshape(piece_rows, head_count, HEAD_DIM),
            preferred_element_type=jnp.float32,
        )
        * scaling
    )
    scores = jnp.where(usable[None, None, :], scores, -1e30)
    peak = jnp.max(scores, axis=2, keepdims=True)
    weights = jnp.where(usable[None, None, :], jnp.exp(scores - peak), 0.0)
    total = jnp.sum(weights, axis=2)
    accum = jnp.einsum(
        "htp,phd->htd",
        weights.astype(jnp.bfloat16),
        piece_values.reshape(piece_rows, head_count, HEAD_DIM),
        preferred_element_type=jnp.float32,
    )
    return (
        (accum / total[:, :, None])
        .transpose(1, 0, 2)
        .reshape(token_count, column_count)
        .astype(jnp.bfloat16)
    )


def pack_by_destination(sources, extra, width):
    ctx_count = extra.shape[0]
    counts = [x.shape[0] for x in sources] + [extra.shape[1]]
    offsets = [sum(counts[:i]) for i in range(len(counts))]
    total_rows = sum(counts)

    def body(*refs):
        out_ref = refs[-1]

        def one(c, carry):
            columns = pl.ds(pl.multiple_of(c * width, width), width)
            for i, ref in enumerate(refs[:-2]):
                out_ref[c, offsets[i] : offsets[i] + counts[i], :] = ref[:, columns]
            out_ref[c, offsets[-1] :, :] = refs[-2][c]
            return carry

        lax.fori_loop(0, ctx_count, one, 0)

    moved = 2 * total_rows * width * ctx_count * extra.dtype.itemsize
    vmem = pl.BlockSpec(memory_space=pltpu.VMEM)
    return pl.pallas_call(
        body,
        in_specs=[vmem] * (len(sources) + 1),
        out_specs=vmem,
        out_shape=jax.ShapeDtypeStruct((ctx_count, total_rows, width), extra.dtype),
        cost_estimate=pl.CostEstimate(flops=0, transcendentals=0, bytes_accessed=moved),
    )(*sources, extra)


def attend_by_head(
    queries, span_keys, span_values, cache_keys, cache_values, length, extra, companion
):
    token_count, column_count = queries.shape
    head_count = column_count // HEAD_DIM
    cached_rows = cache_keys.shape[0]
    ctx_count = lax.axis_size("ctx")
    local_heads = head_count // ctx_count
    width = local_heads * HEAD_DIM
    scaling = 1.0 / math.sqrt(HEAD_DIM)
    block_rows = token_count + cached_rows
    sources = [queries, span_keys, cache_keys, span_values, cache_values]
    base_rows = sum(x.shape[0] for x in sources)
    packed = pack_by_destination(sources, extra, width)
    packed_rows = packed.shape[1]
    got = lax.all_to_all(packed, "ctx", split_axis=0, concat_axis=0, tiled=True)
    got, companion = lax.optimization_barrier((got, companion))
    got = got.reshape(ctx_count, packed_rows, local_heads, HEAD_DIM)
    query_all = got[:, :token_count].reshape(ctx_count * token_count, local_heads, HEAD_DIM)
    key_all = got[:, token_count : token_count + block_rows].reshape(
        ctx_count * block_rows, local_heads, HEAD_DIM
    )
    extra_got = got[:, base_rows:]
    value_all = got[:, token_count + block_rows : base_rows].reshape(
        ctx_count * block_rows, local_heads, HEAD_DIM
    )
    piece_rows = ctx_count * block_rows
    index = jnp.arange(piece_rows, dtype=jnp.int32)
    owner = index // block_rows
    within = index % block_rows
    usable = (within < token_count) | (owner * cached_rows + within - token_count < length)
    scores = (
        jnp.einsum("thd,phd->htp", query_all, key_all, preferred_element_type=jnp.float32)
        * scaling
    )
    scores = jnp.where(usable[None, None, :], scores, -1e30)
    peak = jnp.max(scores, axis=2, keepdims=True)
    weights = jnp.where(usable[None, None, :], jnp.exp(scores - peak), 0.0)
    total = jnp.sum(weights, axis=2)
    accum = jnp.einsum(
        "htp,phd->thd",
        weights.astype(jnp.bfloat16),
        value_all,
        preferred_element_type=jnp.float32,
    )
    head_out = (accum / total.T[:, :, None]).astype(jnp.bfloat16)
    head_out = head_out.reshape(ctx_count, token_count, width)
    back = lax.all_to_all(head_out, "ctx", split_axis=0, concat_axis=0, tiled=True)
    return back.transpose(1, 0, 2).reshape(token_count, column_count), extra_got, companion


def on_device(
    hidden_in,
    queries,
    span_keys,
    span_values,
    cache_keys,
    cache_values,
    cache_lengths,
    slot_request,
    out_weight,
    norm_gain,
    expert_ids,
    expert_gates,
    gate_proj,
    up_proj,
    down_proj,
):
    token_count, feature_width = hidden_in.shape
    column_count = queries.shape[1]
    head_count = column_count // HEAD_DIM
    ctx_count = lax.axis_size("ctx")
    slot_place = lax.axis_index("req")
    slot_count = slot_request.shape[0]
    slot_range = jnp.arange(slot_count, dtype=jnp.int32)
    request = jnp.sum(jnp.where(slot_range == slot_place, slot_request, 0))
    length = jnp.sum(jnp.where(slot_range == request, cache_lengths, 0))
    local_experts = gate_proj.shape[0]
    expert_total = local_experts * ctx_count
    gate_matrix = jnp.sum(
        jnp.where(
            expert_ids[:, :, None] == jnp.arange(expert_total, dtype=jnp.int32)[None, None, :],
            expert_gates[:, :, None],
            0.0,
        ),
        axis=1,
    )
    first_expert = lax.axis_index("ctx") * local_experts
    if head_count % ctx_count == 0:
        width = column_count // ctx_count
        high = lax.reduce_precision(gate_matrix, exponent_bits=8, mantissa_bits=7)
        rest = gate_matrix - high
        middle = lax.reduce_precision(rest, exponent_bits=8, mantissa_bits=7)
        low = rest - middle
        parts = jnp.stack([high, middle, low], 0).astype(jnp.bfloat16)
        parts = parts.reshape(3, token_count, ctx_count, local_experts)
        parts = parts.transpose(2, 0, 3, 1).reshape(ctx_count, -1)
        part_len = parts.shape[1]
        part_rows = -(-part_len // width)
        parts = jnp.pad(parts, ((0, 0), (0, part_rows * width - part_len)))
        parts = parts.reshape(ctx_count, part_rows, width)
        hidden_in = route_to_request(hidden_in, slot_request)
        attended, parts_got, hidden_in = attend_by_head(
            queries, span_keys, span_values, cache_keys, cache_values, length, parts, hidden_in
        )
        carried = jnp.concatenate([attended, parts_got.reshape(-1, column_count)], 0)
        carried = route_to_request(carried, slot_request)
        attended = carried[:token_count]
        parts_got = carried[token_count:]
        routed = True
        parts_got = parts_got.reshape(ctx_count, part_rows * width)[:, :part_len]
        parts_got = parts_got.reshape(ctx_count, 3, local_experts, token_count).astype(
            jnp.float32
        )
        local_gates = (
            (parts_got[:, 0] + parts_got[:, 1]) + parts_got[:, 2]
        ).transpose(1, 0, 2)
    else:
        routed = False
        attended = attend_gathered(
            queries, span_keys, span_values, cache_keys, cache_values, length
        )
        local_gates = lax.all_gather(
            lax.dynamic_slice_in_dim(gate_matrix, first_expert, local_experts, 1).T,
            "ctx",
            axis=1,
            tiled=True,
        ).reshape(local_experts, ctx_count, token_count)
    residual = hidden_in.astype(jnp.float32) + jnp.dot(
        attended, out_weight, preferred_element_type=jnp.float32
    )
    mean_square = jnp.mean(residual * residual, axis=1, keepdims=True)
    normed = (residual * lax.rsqrt(mean_square + 1e-06) * norm_gain).astype(jnp.bfloat16)

    def experts_on(rows, gates):
        moe = None
        for j in range(local_experts):
            gate_val = jnp.dot(rows, gate_proj[j], preferred_element_type=jnp.float32)
            up_val = jnp.dot(rows, up_proj[j], preferred_element_type=jnp.float32)
            activated = (jax.nn.silu(gate_val) * up_val).astype(jnp.bfloat16)
            activated = lax.optimization_barrier(activated)
            produced = jnp.dot(
                activated, down_proj[j], preferred_element_type=jnp.float32
            ).astype(jnp.bfloat16)
            term = gates[j][:, None] * produced.astype(jnp.float32)
            moe = term if moe is None else moe + term
        return moe

    if ctx_count & (ctx_count - 1) == 0 and ctx_count > 1 and token_count % 4 == 0:
        me = lax.axis_index("ctx")
        stream_rows = token_count // 4
        orders = xor_orders(ctx_count)
        moe_pieces = []
        earlier = None
        pending = None
        steps = len(orders[0])
        for group in range(2):
            firsts = [(2 * group + s) * stream_rows for s in range(2)]
            inputs = [normed[f : f + stream_rows] for f in firsts]
            if earlier is not None:
                inputs, _ = lax.optimization_barrier((inputs, earlier))
            helds = gather_xor(inputs, orders, ctx_count)
            earlier = helds
            gates = []
            for first, order in zip(firsts, orders):
                sources = jnp.array(relative_masks(order), jnp.int32) ^ me
                gates.append(
                    jnp.take(
                        local_gates[:, :, first : first + stream_rows], sources, axis=1
                    ).reshape(local_experts, ctx_count * stream_rows)
                )
            rows = jnp.concatenate(
                [held.reshape(ctx_count * stream_rows, feature_width) for held in helds], 0
            )
            if pending is not None:
                rows, pending = lax.optimization_barrier((rows, pending))
                moe_pieces.extend(reduce_xor(pending, orders, ctx_count, steps - 1))
            part = experts_on(rows, jnp.concatenate(gates, 1))
            part = part.reshape(2, ctx_count, stream_rows, feature_width)
            pending = reduce_xor([part[0], part[1]], orders, ctx_count, steps, steps - 1)
        moe_pieces.extend(reduce_xor(pending, orders, ctx_count, steps - 1))
        moe_rows = jnp.concatenate(moe_pieces, 0)
    else:
        normed_all = lax.all_gather(normed, "ctx", axis=0, tiled=True)
        moe = experts_on(normed_all, local_gates.reshape(local_experts, -1))
        moe_rows = lax.psum_scatter(
            moe.astype(jnp.bfloat16), "ctx", scatter_dimension=0, tiled=True
        ).astype(jnp.float32)
    final = (residual + moe_rows).astype(jnp.bfloat16)

    if routed:
        return final
    return route_to_request(final, slot_request)


def xor_orders(ctx_count):
    bits = ctx_count.bit_length() - 1
    first = list(range(bits - 1, -1, -1))
    second = list(first)
    if bits >= 3:
        second[0], second[1] = second[1], second[0]
    return [first, second]


def relative_masks(order):
    return [
        sum(((f >> step) & 1) << bit for step, bit in enumerate(order))
        for f in range(1 << len(order))
    ]


def swap(rows, mask, ctx_count):
    return lax.ppermute(rows, "ctx", [(c, c ^ mask) for c in range(ctx_count)])


def gather_xor(rows_list, orders, ctx_count):
    helds = [rows[None] for rows in rows_list]
    for step in range(len(orders[0])):
        masks = [1 << order[step] for order in orders]
        if all(mask == masks[0] for mask in masks):
            got = swap(jnp.stack(helds), masks[0], ctx_count)
            gots = [got[i] for i in range(len(helds))]
        else:
            gots = [swap(held, mask, ctx_count) for held, mask in zip(helds, masks)]
        helds = [jnp.concatenate([held, got], 0) for held, got in zip(helds, gots)]
        helds = list(lax.optimization_barrier(tuple(helds)))
    return helds


def reduce_xor(parts, orders, ctx_count, start=None, stop=0):
    totals = parts
    start = len(orders[0]) if start is None else start
    for step in reversed(range(stop, start)):
        half = totals[0].shape[0] // 2
        masks = [1 << order[step] for order in orders]
        outgoing = [total[half:].astype(jnp.bfloat16) for total in totals]
        if all(mask == masks[0] for mask in masks):
            sent = swap(jnp.stack(outgoing), masks[0], ctx_count)
            sents = [sent[i] for i in range(len(outgoing))]
        else:
            sents = [swap(out, mask, ctx_count) for out, mask in zip(outgoing, masks)]
        totals = [total[:half] + sent.astype(jnp.float32) for total, sent in zip(totals, sents)]
        totals = list(lax.optimization_barrier(tuple(totals)))
    if stop > 0:
        return totals
    return [total[0] for total in totals]


def route_to_request(final, slot_request):
    slot_count = slot_request.shape[0]
    token_count = final.shape[0]
    slot_range = jnp.arange(slot_count, dtype=jnp.int32)
    if slot_count <= 4:
        orders = list(itertools.permutations(range(slot_count)))
        table = jnp.array(orders, jnp.int32)
        match = jnp.all(table == slot_request[None, :], axis=1)
        choice = jnp.sum(jnp.where(match, jnp.arange(len(orders), dtype=jnp.int32), 0))

        def mover(order):
            pairs = [(g, order[g]) for g in range(slot_count)]
            if all(a == b for a, b in pairs):
                return lambda rows: rows
            return lambda rows: lax.ppermute(rows, "req", pairs)

        return lax.switch(choice, [mover(order) for order in orders], final)
    slot_place = lax.axis_index("req")
    source_slot = jnp.sum(jnp.where(slot_request == slot_place, slot_range, 0))
    piece = lax.all_gather(final, "req", axis=0, tiled=True)
    piece_rows = piece.shape[0]
    offset = source_slot * token_count
    inside = (offset >= 0) & (offset + token_count <= piece_rows)
    portion = lax.dynamic_slice_in_dim(
        piece, jnp.clip(offset, 0, piece_rows - token_count), token_count, 0
    )
    return jnp.where(inside, portion, jnp.zeros_like(final))


def solution(mesh):
    return jax.shard_map(
        on_device,
        mesh=mesh,
        in_specs=(
            P(("req", "ctx"), None),
            P(("req", "ctx"), None),
            P(("req", "ctx"), None),
            P(("req", "ctx"), None),
            P(("req", "ctx"), None),
            P(("req", "ctx"), None),
            P(),
            P(),
            P(),
            P(),
            P(("req", "ctx"), None),
            P(("req", "ctx"), None),
            P("ctx", None, None),
            P("ctx", None, None),
            P("ctx", None, None),
        ),
        out_specs=P(("req", "ctx"), None),
        check_vma=False,
    )
```

profile of v0, /device:TPU:0, one launch (start us, length us, event | category | flops | bytes accessed | tf_op | source)
XLA Modules:
  0.0 142.1 jit_solution(15507369246406583839)
XLA Ops:
  1.4 2.9 %shard_map.271 = bf16[8,774,128]{2,1,0:T(8,128)(2,1)} custom-call(bf16[128,1024]{1,0:T(8,128)(2,1)} %refs_0_.1, bf16[128,1024]{1,0:T(8,128)(2,1)} %refs_1_.1, bf16[192,1024]{1,0:T(8,128)(2,1)} %refs_2_.1, bf16[128,1024]{1,0:T(8,128)(2,1)} %refs_3_.1, bf16[192,1024]{1,0:T(8,128)(2,1)} %refs_4_.1, bf16[8,6,128]{2,1,0:T(8,128)(2,1)} %copy.76.refs_5_), custom_call_target="tpu_custom_call" | custom-call | bytes 3170304 | tf_op jit(solution)/shard_map/pallas_call | solution.py:76
  4.4 5.2 %all-to-all-start = ((bf16[8,774,128]{2,1,0:T(8,128)(2,1)}), bf16[8,774,128]{2,1,0:T(8,128)(2,1)S(1)}, u32[]{:S(2)}, u32[]{:S(2)}) async-start(bf16[8,774,128]{2,1,0:T(8,128)(2,1)} %shard_map.271), calls=%async_computation | async-start | bytes 3178496 | tf_op jit(solution)/shard_map/all_to_all | solution.py:100
  11.0 16.3 %conditional.2 = (bf16[128,2048]{1,0:T(8,128)(2,1)S(1)}) conditional(s32[]{:T(128)} %clamp.6, bf16[128,2048]{1,0:T(8,128)(2,1)S(1)} %copy-done.1, bf16[128,2048]{1,0:T(8,128)(2,1)S(1)} %copy-done.1, bf16[128,2048]{1,0:T(8,128)(2,1)S(1)} %copy-done.1, bf16[128,2048]{1,0:T(8,128)(2,1)S(1)} %copy-done.1, ...), branch_computations={%region_3.4_spmd, %region_4.5_spmd, %region_5.6_spmd, %region_6.7_... | conditional | bytes 3145776 | solution.py:349
  11.0 1.6 %collective-permute-start.8 = (bf16[128,2048]{1,0:T(8,128)(2,1)S(1)}, bf16[128,2048]{1,0:T(8,128)(2,1)S(1)}, u32[]{:S(2)}, u32[]{:S(2)}) collective-permute-start(bf16[128,2048]{1,0:T(8,128)(2,1)S(1)} %param.9), channel_id=1, source_target_pairs={{0,8},{8,16},{16,24},{24,0},{1,9},{9,17},{17,25},{25,1},{2,10},{10... | collective-permute-start | bytes 1572872 | tf_op jit(solution)/shard_map/cond/branch_9_fun/ppermute | solution.py:347
  12.6 14.6 %collective-permute-done.8 = bf16[128,2048]{1,0:T(8,128)(2,1)S(1)} collective-permute-done((bf16[128,2048]{1,0:T(8,128)(2,1)S(1)}, bf16[128,2048]{1,0:T(8,128)(2,1)S(1)}, u32[]{:S(2)}, u32[]{:S(2)}) %collective-permute-start.8) | collective-permute-done | bytes 524320 | tf_op jit(solution)/shard_map/cond/branch_9_fun/ppermute | solution.py:347
  30.9 1.8 %fusion = (f32[1024]{0:T(1024)S(1)}, f32[1024,2560]{1,0:T(8,128)S(1)}) fusion(pred[2560]{0:T(1024)(128)(4,1)S(1)} %fusion.86, bf16[1024,128]{1,0:T(8,128)(2,1)S(1)} %bitcast.194, bf16[2560,128]{1,0:T(8,128)(2,1)S(1)} %bitcast.189), kind=kOutput, calls=%fused_computation.6 | convolution fusion | flops 678951936 | bytes 11409920 | tf_op jit(solution)/shard_map/thd,phd->htp/dot_general | solution.py:117
  32.7 2.7 %fusion.1 = f32[1024]{0:T(1024)S(1)} fusion(f32[1024,2560]{1,0:T(8,128)S(1)} %get-tuple-element.208, f32[1024]{0:T(1024)S(1)} %get-tuple-element.207, pred[2560]{0:T(1024)(128)(4,1)S(1)} %fusion.86), kind=kLoop, calls=%fused_computation.7 | loop fusion | flops 13106176 | bytes 10496512 | tf_op jit(solution)/shard_map/reduce_sum | solution.py:123
  35.4 3.0 %fusion.72 = bf16[16,8,8,128]{3,1,2,0:T(8,128)(2,1)S(1)} fusion(bf16[2560,128]{1,0:T(8,128)(2,1)S(1)} %bitcast.209, f32[1024,2560]{1,0:T(8,128)S(1)} %get-tuple-element.208, f32[1024]{0:T(1024)S(1)} %get-tuple-element.207, pred[2560]{0:T(1024)(128)(4,1)S(1)} %fusion.86, f32[1024]{0:T(1024)S(1)} %fusion.1), kind=kOutput, calls=%fused_computation.79 | convolution fusion | flops 684457984 | bytes 11414016 | tf_op jit(solution)/shard_map/htp,phd->thd/dot_general | solution.py:124
  39.3 3.4 %all-to-all-start.1 = ((bf16[8,128,128]{1,2,0:T(8,128)(2,1)}), bf16[8,128,128]{1,2,0:T(8,128)(2,1)S(1)}, u32[]{:S(2)}, u32[]{:S(2)}) async-start(bf16[8,128,128]{1,2,0:T(8,128)(2,1)} %copy.77), calls=%async_computation.1 | async-start | bytes 524288 | tf_op jit(solution)/shard_map/all_to_all | solution.py:132
  42.8 6.7 %all-to-all-done.1 = bf16[8,128,128]{1,2,0:T(8,128)(2,1)S(1)} async-done(((bf16[8,128,128]{1,2,0:T(8,128)(2,1)}), bf16[8,128,128]{1,2,0:T(8,128)(2,1)S(1)}, u32[]{:S(2)}, u32[]{:S(2)}) %all-to-all-start.1) | async-done | bytes 262176 | tf_op jit(solution)/shard_map/all_to_all | solution.py:132
  49.7 9.9 %conditional.3 = (bf16[134,1024]{1,0:T(8,128)(2,1)S(1)}) conditional(s32[]{:T(128)} %clamp.6, bf16[134,1024]{1,0:T(8,128)(2,1)S(1)} %pad_maximum_fusion.14, bf16[134,1024]{1,0:T(8,128)(2,1)S(1)} %pad_maximum_fusion.14, bf16[134,1024]{1,0:T(8,128)(2,1)S(1)} %pad_maximum_fusion.14, ...), branch_computations={%region_33.34_spmd, %region_34.35_spmd, %region_35.36_spmd, %regio... | conditional | bytes 1646640 | solution.py:349
  49.8 1.6 %collective-permute-start.31 = (bf16[134,1024]{1,0:T(8,128)(2,1)S(1)}, bf16[134,1024]{1,0:T(8,128)(2,1)S(1)}, u32[]{:S(2)}, u32[]{:S(2)}) collective-permute-start(bf16[134,1024]{1,0:T(8,128)(2,1)S(1)} %param.33), channel_id=1, source_target_pairs={{0,8},{8,16},{16,24},{24,0},{1,9},{9,17},{17,25},{25,1},{2,10},{10... | collective-permute-start | bytes 823304 | tf_op jit(solution)/shard_map/cond/branch_9_fun/ppermute | solution.py:347
  51.4 8.0 %collective-permute-done.31 = bf16[134,1024]{1,0:T(8,128)(2,1)S(1)} collective-permute-done((bf16[134,1024]{1,0:T(8,128)(2,1)S(1)}, bf16[134,1024]{1,0:T(8,128)(2,1)S(1)}, u32[]{:S(2)}, u32[]{:S(2)}) %collective-permute-start.31) | collective-permute-done | bytes 274464 | tf_op jit(solution)/shard_map/cond/branch_9_fun/ppermute | solution.py:347
  59.7 3.0 %multiply_reduce_fusion = (f32[128]{0:T(128)S(1)}, f32[128,2048]{1,0:T(8,128)S(1)}) fusion(bf16[1024,2048]{1,0:T(8,128)(2,1)} %param.79, bf16[134,1024]{1,0:T(8,128)(2,1)S(1)} %get-tuple-element.220, bf16[128,2048]{1,0:T(8,128)(2,1)S(1)} %get-tuple-element.219), kind=kOutput, calls=%fused_computation.76 | convolution fusion | flops 537919360 | bytes 6029824 | tf_op jit(solution)/shard_map/dot_general | solution.py:213
  64.7 3.2 %collective-permute-done.46 = bf16[1,32,2048]{2,1,0:T(8,128)(2,1)S(1)} collective-permute-done((bf16[1,32,2048]{2,1,0:T(8,128)(2,1)S(1)}, bf16[1,32,2048]{2,1,0:T(8,128)(2,1)S(1)}, u32[]{:S(2)}, u32[]{:S(2)}) %collective-permute-start.46) | collective-permute-done | bytes 131104 | tf_op jit(solution)/shard_map/ppermute | solution.py:297
  71.0 1.7 %collective-permute-start.49 = (bf16[2,32,2048]{2,1,0:T(8,128)(2,1)S(1)}, bf16[2,32,2048]{2,1,0:T(8,128)(2,1)S(1)}, u32[]{:S(2)}, u32[]{:S(2)}) collective-permute-start(bf16[2,32,2048]{2,1,0:T(8,128)(2,1)S(1)} %pad_maximum_fusion.16), channel_id=1, source_target_pairs={{0,4},{1,5},{2,6},{3,7},{4,0},{5,1},{6,2},{7,3},{8,12},{9,13},{10,... | collective-permute-start | bytes 786440 | tf_op jit(solution)/shard_map/ppermute | solution.py:297
  75.2 2.2 %collective-permute-done.49 = bf16[2,32,2048]{2,1,0:T(8,128)(2,1)S(1)} collective-permute-done((bf16[2,32,2048]{2,1,0:T(8,128)(2,1)S(1)}, bf16[2,32,2048]{2,1,0:T(8,128)(2,1)S(1)}, u32[]{:S(2)}, u32[]{:S(2)}) %collective-permute-start.49) | collective-permute-done | bytes 262176 | tf_op jit(solution)/shard_map/ppermute | solution.py:297
  79.0 2.5 %collective-permute-done.50 = bf16[2,4,32,2048]{3,2,1,0:T(8,128)(2,1)S(1)} collective-permute-done((bf16[2,4,32,2048]{3,2,1,0:T(8,128)(2,1)}, bf16[2,4,32,2048]{3,2,1,0:T(8,128)(2,1)S(1)}, u32[]{:S(2)}, u32[]{:S(2)}) %collective-permute-start.50) | collective-permute-done | bytes 1048608 | tf_op jit(solution)/shard_map/ppermute | solution.py:297
  84.2 1.7 %collective-permute-start.51 = (bf16[1,32,2048]{2,1,0:T(8,128)(2,1)S(1)}, bf16[1,32,2048]{2,1,0:T(8,128)(2,1)S(1)}, u32[]{:S(2)}, u32[]{:S(2)}) collective-permute-start(bf16[1,32,2048]{2,1,0:T(8,128)(2,1)S(1)} %bitcast.212), channel_id=1, source_target_pairs={{0,4},{1,5},{2,6},{3,7},{4,0},{5,1},{6,2},{7,3},{8,12},{9,13},{10,... | collective-permute-start | bytes 393224 | tf_op jit(solution)/shard_map/ppermute | solution.py:297
  86.7 1.3 fusion.53
  88.1 1.4 fusion.59
  91.5 1.4 %fusion.104 = (bf16[512,2048]{1,0:T(8,128)(2,1)S(1)}, f32[512,2048]{1,0:T(8,128)S(1)}) fusion(bf16[512,512]{1,0:T(8,128)(2,1)S(1)} %fusion.53, bf16[2,512,2048]{2,1,0:T(8,128)(2,1)S(1)} %copy-done, f32[512]{0:T(512)S(1)} %bitcast.217, bf16[512,2048]{1,0:T(8,128)(2,1)S(1)} %convolution_convert_fusion.3, f32[512]{0:T(512)S(1)} %bitcast.216), kind=kOutput, calls=%fused_computation.179 | convolution fusion | flops 1081081856 | bytes 11014144 | tf_op jit(solution)/shard_map/dot_general | solution.py:226
  93.1 1.4 collective-permute-start.53
  95.2 5.7 %collective-permute-done.53 = bf16[2,32,2048]{2,1,0:T(8,128)(2,1)S(1)} collective-permute-done((bf16[2,32,2048]{2,1,0:T(8,128)(2,1)S(1)}, bf16[2,32,2048]{2,1,0:T(8,128)(2,1)S(1)}, u32[]{:S(2)}, u32[]{:S(2)}) %collective-permute-start.53) | collective-permute-done | bytes 262176 | tf_op jit(solution)/shard_map/ppermute | solution.py:297
  102.9 2.1 %collective-permute-done.55 = bf16[2,4,32,2048]{3,2,1,0:T(8,128)(2,1)S(1)} collective-permute-done((bf16[2,4,32,2048]{3,2,1,0:T(8,128)(2,1)S(1)}, bf16[2,4,32,2048]{3,2,1,0:T(8,128)(2,1)S(1)}, u32[]{:S(2)}, u32[]{:S(2)}) %collective-permute-start.55) | collective-permute-done | bytes 1048608 | tf_op jit(solution)/shard_map/ppermute | solution.py:297
  108.0 1.3 fusion.50
  109.3 1.6 %fusion.56 = bf16[512,512]{1,0:T(8,128)(2,1)S(1)} fusion(bf16[512,2048]{1,0:T(8,128)(2,1)S(1)} %pad_maximum_fusion, bf16[2,2048,512]{2,1,0:T(8,128)(2,1)S(1)} %copy-done.8, f32[512,512]{1,0:T(8,128)S(1)} %fusion.22), kind=kOutput, calls=%fused_computation.58 | convolution fusion | flops 1075314688 | bytes 5767168 | tf_op jit(solution)/shard_map/dot_general | solution.py:223
  112.2 1.4 %fusion.105 = (bf16[512,2048]{1,0:T(8,128)(2,1)S(1)}, f32[512,2048]{1,0:T(8,128)S(1)}) fusion(bf16[512,512]{1,0:T(8,128)(2,1)S(1)} %fusion.50, bf16[2,512,2048]{2,1,0:T(8,128)(2,1)S(1)} %copy-done, f32[512]{0:T(512)S(1)} %bitcast.215, bf16[512,2048]{1,0:T(8,128)(2,1)S(1)} %convolution_convert_fusion.1, f32[512]{0:T(512)S(1)} %bitcast.214), kind=kOutput, calls=%fused_computation.180 | convolution fusion | flops 1081081856 | bytes 11014144 | tf_op jit(solution)/shard_map/dot_general | solution.py:226
  116.0 6.8 %collective-permute-done.57 = bf16[2,32,2048]{2,1,0:T(8,128)(2,1)S(1)} collective-permute-done((bf16[2,32,2048]{2,1,0:T(8,128)(2,1)S(1)}, bf16[2,32,2048]{2,1,0:T(8,128)(2,1)S(1)}, u32[]{:S(2)}, u32[]{:S(2)}) %collective-permute-start.57) | collective-permute-done | bytes 262176 | tf_op jit(solution)/shard_map/ppermute | solution.py:297
  127.0 1.6 %collective-permute-done.59 = bf16[1,32,2048]{2,1,0:T(8,128)(2,1)S(1)} collective-permute-done((bf16[1,32,2048]{2,1,0:T(8,128)(2,1)S(1)}, bf16[1,32,2048]{2,1,0:T(8,128)(2,1)S(1)}, u32[]{:S(2)}, u32[]{:S(2)}) %collective-permute-start.59) | collective-permute-done | bytes 131104 | tf_op jit(solution)/shard_map/ppermute | solution.py:297
  129.5 5.0 %collective-permute-done.62 = bf16[2,32,2048]{2,1,0:T(8,128)(2,1)S(1)} collective-permute-done((bf16[2,32,2048]{2,1,0:T(8,128)(2,1)S(1)}, bf16[2,32,2048]{2,1,0:T(8,128)(2,1)S(1)}, u32[]{:S(2)}, u32[]{:S(2)}) %collective-permute-start.62) | collective-permute-done | bytes 262176 | tf_op jit(solution)/shard_map/ppermute | solution.py:297
  137.4 2.9 %collective-permute-done.64 = bf16[1,32,2048]{2,1,0:T(8,128)(2,1)S(1)} collective-permute-done((bf16[1,32,2048]{2,1,0:T(8,128)(2,1)S(1)}, bf16[1,32,2048]{2,1,0:T(8,128)(2,1)S(1)}, u32[]{:S(2)}, u32[]{:S(2)}) %collective-permute-start.64) | collective-permute-done | bytes 131104 | tf_op jit(solution)/shard_map/ppermute | solution.py:297
  (145 shorter events, 40.6 us)
Async XLA Ops:
  0.0 9.6 %copy-start.3 = (s32[24,4]{0,1:T(4,128)S(1)}, s32[24,4]{0,1:T(4,128)}, u32[]{:S(2)}) copy-start(s32[24,4]{0,1:T(4,128)} %constant.74.clone) | copy-start | bytes 1156
  0.0 10.3 %copy-start.1 = (bf16[128,2048]{1,0:T(8,128)(2,1)S(1)}, bf16[128,2048]{1,0:T(8,128)(2,1)}, u32[]{:S(2)}) copy-start(bf16[128,2048]{1,0:T(8,128)(2,1)} %param.71) | copy-start | bytes 1572868
  0.0 9.6 %copy-start.6 = (s32[4]{0:T(128)S(1)}, s32[4]{0:T(128)}, u32[]{:S(2)}) copy-start(s32[4]{0:T(128)} %param.78) | copy-start | bytes 52
  4.4 26.4 %all-to-all-start = ((bf16[8,774,128]{2,1,0:T(8,128)(2,1)}), bf16[8,774,128]{2,1,0:T(8,128)(2,1)S(1)}, u32[]{:S(2)}, u32[]{:S(2)}) async-start(bf16[8,774,128]{2,1,0:T(8,128)(2,1)} %shard_map.271), calls=%async_computation | async-start | bytes 3178496 | tf_op jit(solution)/shard_map/all_to_all | solution.py:100
  10.9 17.0 %copy-start.9 = (s32[4]{0:T(128)S(1)}, s32[4]{0:T(128)}, u32[]{:S(2)}) copy-start(s32[4]{0:T(128)} %param.77) | copy-start | bytes 52
  11.0 16.2 %collective-permute-start.8 = (bf16[128,2048]{1,0:T(8,128)(2,1)S(1)}, bf16[128,2048]{1,0:T(8,128)(2,1)S(1)}, u32[]{:S(2)}, u32[]{:S(2)}) collective-permute-start(bf16[128,2048]{1,0:T(8,128)(2,1)S(1)} %param.9), channel_id=1, source_target_pairs={{0,8},{8,16},{16,24},{24,0},{1,9},{9,17},{17,25},{25,1},{2,10},{10... | collective-permute-start | bytes 1572872 | tf_op jit(solution)/shard_map/cond/branch_9_fun/ppermute | solution.py:347
  35.4 7.3 %copy-start.4 = (s32[8]{0:T(128)S(1)}, s32[8]{0:T(128)}, u32[]{:S(2)}) copy-start(s32[8]{0:T(128)} %constant.76.clone) | copy-start | bytes 100
  35.4 7.3 %copy-start.5 = (s32[8]{0:T(128)S(1)}, s32[8]{0:T(128)}, u32[]{:S(2)}) copy-start(s32[8]{0:T(128)} %constant.75.clone) | copy-start | bytes 100
  39.3 10.3 %all-to-all-start.1 = ((bf16[8,128,128]{1,2,0:T(8,128)(2,1)}), bf16[8,128,128]{1,2,0:T(8,128)(2,1)S(1)}, u32[]{:S(2)}, u32[]{:S(2)}) async-start(bf16[8,128,128]{1,2,0:T(8,128)(2,1)} %copy.77), calls=%async_computation.1 | async-start | bytes 524288 | tf_op jit(solution)/shard_map/all_to_all | solution.py:132
  49.8 9.7 %collective-permute-start.31 = (bf16[134,1024]{1,0:T(8,128)(2,1)S(1)}, bf16[134,1024]{1,0:T(8,128)(2,1)S(1)}, u32[]{:S(2)}, u32[]{:S(2)}) collective-permute-start(bf16[134,1024]{1,0:T(8,128)(2,1)S(1)} %param.33), channel_id=1, source_target_pairs={{0,8},{8,16},{16,24},{24,0},{1,9},{9,17},{17,25},{25,1},{2,10},{10... | collective-permute-start | bytes 823304 | tf_op jit(solution)/shard_map/cond/branch_9_fun/ppermute | solution.py:347
  59.6 3.1 %copy-start.2 = (f32[2048]{0:T(1024)S(1)}, f32[2048]{0:T(1024)}, u32[]{:S(2)}) copy-start(f32[2048]{0:T(1024)} %param.80) | copy-start | bytes 24580
  62.9 5.0 %collective-permute-start.46 = (bf16[1,32,2048]{2,1,0:T(8,128)(2,1)S(1)}, bf16[1,32,2048]{2,1,0:T(8,128)(2,1)S(1)}, u32[]{:S(2)}, u32[]{:S(2)}) collective-permute-start(bf16[1,32,2048]{2,1,0:T(8,128)(2,1)S(1)} %get-tuple-element.189), channel_id=1, source_target_pairs={{0,4},{1,5},{2,6},{3,7},{4,0},{5,1},{6,2},{7,3},{8,12},{9,13},{10,... | collective-permute-start | bytes 393224 | tf_op jit(solution)/shard_map/ppermute | solution.py:297
  63.5 5.2 %collective-permute-start.47 = (bf16[1,32,2048]{2,1,0:T(8,128)(2,1)S(1)}, bf16[1,32,2048]{2,1,0:T(8,128)(2,1)S(1)}, u32[]{:S(2)}, u32[]{:S(2)}) collective-permute-start(bf16[1,32,2048]{2,1,0:T(8,128)(2,1)S(1)} %get-tuple-element.188), channel_id=1, source_target_pairs={{0,2},{1,3},{2,0},{3,1},{4,6},{5,7},{6,4},{7,5},{8,10},{9,11},{10,... | collective-permute-start | bytes 393224 | tf_op jit(solution)/shard_map/ppermute | solution.py:297
  68.7 6.4 %collective-permute-start.48 = (bf16[2,32,2048]{2,1,0:T(8,128)(2,1)S(1)}, bf16[2,32,2048]{2,1,0:T(8,128)(2,1)S(1)}, u32[]{:S(2)}, u32[]{:S(2)}) collective-permute-start(bf16[2,32,2048]{2,1,0:T(8,128)(2,1)S(1)} %pad_maximum_fusion.15), channel_id=1, source_target_pairs={{0,2},{1,3},{2,0},{3,1},{4,6},{5,7},{6,4},{7,5},{8,10},{9,11},{10,... | collective-permute-start | bytes 786440 | tf_op jit(solution)/shard_map/ppermute | solution.py:297
  71.0 6.4 %collective-permute-start.49 = (bf16[2,32,2048]{2,1,0:T(8,128)(2,1)S(1)}, bf16[2,32,2048]{2,1,0:T(8,128)(2,1)S(1)}, u32[]{:S(2)}, u32[]{:S(2)}) collective-permute-start(bf16[2,32,2048]{2,1,0:T(8,128)(2,1)S(1)} %pad_maximum_fusion.16), channel_id=1, source_target_pairs={{0,4},{1,5},{2,6},{3,7},{4,0},{5,1},{6,2},{7,3},{8,12},{9,13},{10,... | collective-permute-start | bytes 786440 | tf_op jit(solution)/shard_map/ppermute | solution.py:297
  78.6 2.9 %collective-permute-start.50 = (bf16[2,4,32,2048]{3,2,1,0:T(8,128)(2,1)}, bf16[2,4,32,2048]{3,2,1,0:T(8,128)(2,1)S(1)}, u32[]{:S(2)}, u32[]{:S(2)}) collective-permute-start(bf16[2,4,32,2048]{3,2,1,0:T(8,128)(2,1)} %pad_maximum_fusion.2), channel_id=1, source_target_pairs={{0,1},{1,0},{2,3},{3,2},{4,5},{5,4},{6,7},{7,6},{8,9},{9,8},{10,11... | collective-permute-start | bytes 3145736 | tf_op jit(solution)/shard_map/ppermute | solution.py:297
  83.0 3.7 %copy-start.8 = (bf16[2,2048,512]{2,1,0:T(8,128)(2,1)S(1)}, bf16[2,2048,512]{2,1,0:T(8,128)(2,1)}, u32[]{:S(2)}) copy-start(bf16[2,2048,512]{2,1,0:T(8,128)(2,1)} %param.84) | copy-start | bytes 12582916
  84.2 8.7 %collective-permute-start.51 = (bf16[1,32,2048]{2,1,0:T(8,128)(2,1)S(1)}, bf16[1,32,2048]{2,1,0:T(8,128)(2,1)S(1)}, u32[]{:S(2)}, u32[]{:S(2)}) collective-permute-start(bf16[1,32,2048]{2,1,0:T(8,128)(2,1)S(1)} %bitcast.212), channel_id=1, source_target_pairs={{0,4},{1,5},{2,6},{3,7},{4,0},{5,1},{6,2},{7,3},{8,12},{9,13},{10,... | collective-permute-start | bytes 393224 | tf_op jit(solution)/shard_map/ppermute | solution.py:297
  86.0 7.1 %collective-permute-start.52 = (bf16[1,32,2048]{2,1,0:T(8,128)(2,1)S(1)}, bf16[1,32,2048]{2,1,0:T(8,128)(2,1)S(1)}, u32[]{:S(2)}, u32[]{:S(2)}) collective-permute-start(bf16[1,32,2048]{2,1,0:T(8,128)(2,1)S(1)} %bitcast.210), channel_id=1, source_target_pairs={{0,2},{1,3},{2,0},{3,1},{4,6},{5,7},{6,4},{7,5},{8,10},{9,11},{10,... | collective-permute-start | bytes 393224 | tf_op jit(solution)/shard_map/ppermute | solution.py:297
  93.1 7.8 %collective-permute-start.53 = (bf16[2,32,2048]{2,1,0:T(8,128)(2,1)S(1)}, bf16[2,32,2048]{2,1,0:T(8,128)(2,1)S(1)}, u32[]{:S(2)}, u32[]{:S(2)}) collective-permute-start(bf16[2,32,2048]{2,1,0:T(8,128)(2,1)S(1)} %pad_maximum_fusion.17), channel_id=1, source_target_pairs={{0,2},{1,3},{2,0},{3,1},{4,6},{5,7},{6,4},{7,5},{8,10},{9,11},{10,... | collective-permute-start | bytes 786440 | tf_op jit(solution)/shard_map/ppermute | solution.py:297
  94.5 7.6 %collective-permute-start.54 = (bf16[2,32,2048]{2,1,0:T(8,128)(2,1)S(1)}, bf16[2,32,2048]{2,1,0:T(8,128)(2,1)S(1)}, u32[]{:S(2)}, u32[]{:S(2)}) collective-permute-start(bf16[2,32,2048]{2,1,0:T(8,128)(2,1)S(1)} %pad_maximum_fusion.18), channel_id=1, source_target_pairs={{0,4},{1,5},{2,6},{3,7},{4,0},{5,1},{6,2},{7,3},{8,12},{9,13},{10,... | collective-permute-start | bytes 786440 | tf_op jit(solution)/shard_map/ppermute | solution.py:297
  95.1 7.5 %collective-permute-start.56 = (bf16[2,4,32,2048]{3,2,1,0:T(8,128)(2,1)S(1)}, bf16[2,4,32,2048]{3,2,1,0:T(8,128)(2,1)S(1)}, u32[]{:S(2)}, u32[]{:S(2)}) collective-permute-start(bf16[2,4,32,2048]{3,2,1,0:T(8,128)(2,1)S(1)} %pad_maximum_fusion.8), channel_id=1, source_target_pairs={{0,1},{1,0},{2,3},{3,2},{4,5},{5,4},{6,7},{7,6},{8,9},{9,8},{10,11... | collective-permute-start | bytes 3145736 | tf_op jit(solution)/shard_map/ppermute | solution.py:297
  102.3 2.7 %collective-permute-start.55 = (bf16[2,4,32,2048]{3,2,1,0:T(8,128)(2,1)S(1)}, bf16[2,4,32,2048]{3,2,1,0:T(8,128)(2,1)S(1)}, u32[]{:S(2)}, u32[]{:S(2)}) collective-permute-start(bf16[2,4,32,2048]{3,2,1,0:T(8,128)(2,1)S(1)} %pad_maximum_fusion.5), channel_id=1, source_target_pairs={{0,1},{1,0},{2,3},{3,2},{4,5},{5,4},{6,7},{7,6},{8,9},{9,8},{10,11... | collective-permute-start | bytes 3145736 | tf_op jit(solution)/shard_map/ppermute | solution.py:297
  113.8 11.6 %collective-permute-start.61 = (bf16[2,4,32,2048]{3,2,1,0:T(8,128)(2,1)S(1)}, bf16[2,4,32,2048]{3,2,1,0:T(8,128)(2,1)S(1)}, u32[]{:S(2)}, u32[]{:S(2)}) collective-permute-start(bf16[2,4,32,2048]{3,2,1,0:T(8,128)(2,1)S(1)} %pad_maximum_fusion.9), channel_id=1, source_target_pairs={{0,1},{1,0},{2,3},{3,2},{4,5},{5,4},{6,7},{7,6},{8,9},{9,8},{10,11... | collective-permute-start | bytes 3145736 | tf_op jit(solution)/shard_map/ppermute | solution.py:297
  114.1 8.7 %collective-permute-start.57 = (bf16[2,32,2048]{2,1,0:T(8,128)(2,1)S(1)}, bf16[2,32,2048]{2,1,0:T(8,128)(2,1)S(1)}, u32[]{:S(2)}, u32[]{:S(2)}) collective-permute-start(bf16[2,32,2048]{2,1,0:T(8,128)(2,1)S(1)} %slice.460), channel_id=1, source_target_pairs={{0,2},{1,3},{2,0},{3,1},{4,6},{5,7},{6,4},{7,5},{8,10},{9,11},{10,... | collective-permute-start | bytes 786440 | tf_op jit(solution)/shard_map/ppermute | solution.py:297
  115.1 8.4 %collective-permute-start.58 = (bf16[2,32,2048]{2,1,0:T(8,128)(2,1)S(1)}, bf16[2,32,2048]{2,1,0:T(8,128)(2,1)S(1)}, u32[]{:S(2)}, u32[]{:S(2)}) collective-permute-start(bf16[2,32,2048]{2,1,0:T(8,128)(2,1)S(1)} %slice.459), channel_id=1, source_target_pairs={{0,4},{1,5},{2,6},{3,7},{4,0},{5,1},{6,2},{7,3},{8,12},{9,13},{10,... | collective-permute-start | bytes 786440 | tf_op jit(solution)/shard_map/ppermute | solution.py:297
  123.6 5.0 %collective-permute-start.59 = (bf16[1,32,2048]{2,1,0:T(8,128)(2,1)S(1)}, bf16[1,32,2048]{2,1,0:T(8,128)(2,1)S(1)}, u32[]{:S(2)}, u32[]{:S(2)}) collective-permute-start(bf16[1,32,2048]{2,1,0:T(8,128)(2,1)S(1)} %slice.464), channel_id=1, source_target_pairs={{0,4},{1,5},{2,6},{3,7},{4,0},{5,1},{6,2},{7,3},{8,12},{9,13},{10,... | collective-permute-start | bytes 393224 | tf_op jit(solution)/shard_map/ppermute | solution.py:297
  124.4 11.6 %collective-permute-start.60 = (bf16[1,32,2048]{2,1,0:T(8,128)(2,1)S(1)}, bf16[1,32,2048]{2,1,0:T(8,128)(2,1)S(1)}, u32[]{:S(2)}, u32[]{:S(2)}) collective-permute-start(bf16[1,32,2048]{2,1,0:T(8,128)(2,1)S(1)} %slice.463), channel_id=1, source_target_pairs={{0,2},{1,3},{2,0},{3,1},{4,6},{5,7},{6,4},{7,5},{8,10},{9,11},{10,... | collective-permute-start | bytes 393224 | tf_op jit(solution)/shard_map/ppermute | solution.py:297
  125.8 8.6 %collective-permute-start.62 = (bf16[2,32,2048]{2,1,0:T(8,128)(2,1)S(1)}, bf16[2,32,2048]{2,1,0:T(8,128)(2,1)S(1)}, u32[]{:S(2)}, u32[]{:S(2)}) collective-permute-start(bf16[2,32,2048]{2,1,0:T(8,128)(2,1)S(1)} %slice.458), channel_id=1, source_target_pairs={{0,2},{1,3},{2,0},{3,1},{4,6},{5,7},{6,4},{7,5},{8,10},{9,11},{10,... | collective-permute-start | bytes 786440 | tf_op jit(solution)/shard_map/ppermute | solution.py:297
  128.7 6.4 %collective-permute-start.63 = (bf16[2,32,2048]{2,1,0:T(8,128)(2,1)S(1)}, bf16[2,32,2048]{2,1,0:T(8,128)(2,1)S(1)}, u32[]{:S(2)}, u32[]{:S(2)}) collective-permute-start(bf16[2,32,2048]{2,1,0:T(8,128)(2,1)S(1)} %slice.457), channel_id=1, source_target_pairs={{0,4},{1,5},{2,6},{3,7},{4,0},{5,1},{6,2},{7,3},{8,12},{9,13},{10,... | collective-permute-start | bytes 786440 | tf_op jit(solution)/shard_map/ppermute | solution.py:297
  135.2 5.0 %collective-permute-start.64 = (bf16[1,32,2048]{2,1,0:T(8,128)(2,1)S(1)}, bf16[1,32,2048]{2,1,0:T(8,128)(2,1)S(1)}, u32[]{:S(2)}, u32[]{:S(2)}) collective-permute-start(bf16[1,32,2048]{2,1,0:T(8,128)(2,1)S(1)} %slice.462), channel_id=1, source_target_pairs={{0,4},{1,5},{2,6},{3,7},{4,0},{5,1},{6,2},{7,3},{8,12},{9,13},{10,... | collective-permute-start | bytes 393224 | tf_op jit(solution)/shard_map/ppermute | solution.py:297
  136.1 5.0 %collective-permute-start.65 = (bf16[1,32,2048]{2,1,0:T(8,128)(2,1)S(1)}, bf16[1,32,2048]{2,1,0:T(8,128)(2,1)S(1)}, u32[]{:S(2)}, u32[]{:S(2)}) collective-permute-start(bf16[1,32,2048]{2,1,0:T(8,128)(2,1)S(1)} %slice.461), channel_id=1, source_target_pairs={{0,2},{1,3},{2,0},{3,1},{4,6},{5,7},{6,4},{7,5},{8,10},{9,11},{10,... | collective-permute-start | bytes 393224 | tf_op jit(solution)/shard_map/ppermute | solution.py:297
  (2 other events, 5.0 us)
where the time goes:
time: 144 us; the launch traced here: 142 us
  waiting for transfers between devices  67.5 us (47%)
  starting transfers between devices  28.4 us (20%)
  matrix products  23.9 us (17%)
  other arithmetic  11.4 us (8%)
  local copies, waits for them, and re-layouts  6.42 us (4%)
  Pallas kernels  2.94 us (2%)
    ppermute x20, waiting for transfers between devices, swap(): return lax.ppermute(rows, 'ctx', [(c, c ^ mask) for c in range(ctx_count)])  37.2 us
    ppermute x2, waiting for transfers between devices, mover(): return lambda rows: lax.ppermute(rows, 'req', pairs)  22.6 us
    ppermute x20, starting transfers between devices, swap(): return lax.ppermute(rows, 'ctx', [(c, c ^ mask) for c in range(ctx_count)])  16.6 us
    all_to_all x1, waiting for transfers between devices, attend_by_head(): lax.all_to_all(head_out, 'ctx', split_axis=0, concat_axis=0, tiled=True)  6.75 us
    dot_general x4, matrix products, experts_on(): up_val = jnp.dot(rows, up_proj[j], preferred_element_type=jnp.float32)  5.59 us
    dot_general x4, matrix products, experts_on(): jnp.dot(activated, down_proj[j], preferred_element_type=jnp.float32)  5.42 us
    all_to_all x1, starting transfers between devices, attend_by_head(): got = lax.all_to_all(packed, 'ctx', split_axis=0, concat_axis=0, tiled=True)  5.17 us
    dot_general x4, matrix products, experts_on(): gate_val = jnp.dot(rows, gate_proj[j], preferred_element_type=jnp.float32)  5.02 us
  transfers between devices with their start and end apart: 24, of which 19 were waited for; matrix products, arithmetic and copies ran while one was open for 10% of the time, Pallas kernels for 0%

commit v1 on v0

--- a/solution.py
+++ b/solution.py
@@ -82,6 +82,51 @@
     )(*sources, extra)
 
 
+def attend_one_head(query, key, value, usable_row):
+    rows, depth = query.shape
+    keys = key.shape[0]
+    block = 256 if rows % 256 == 0 else rows
+    scaling = 1.0 / math.sqrt(HEAD_DIM)
+
+    def body(q_ref, k_ref, v_ref, m_ref, o_ref):
+        scores = (
+            lax.dot_general(
+                q_ref[...],
+                k_ref[...],
+                (((1,), (1,)), ((), ())),
+                preferred_element_type=jnp.float32,
+            )
+            * scaling
+        )
+        usable = m_ref[...] != 0
+        scores = jnp.where(usable, scores, -1e30)
+        peak = jnp.max(scores, axis=1, keepdims=True)
+        weights = jnp.where(usable, jnp.exp(scores - peak), 0.0)
+        total = jnp.sum(weights, axis=1, keepdims=True)
+        accum = jnp.dot(
+            weights.astype(jnp.bfloat16), v_ref[...], preferred_element_type=jnp.float32
+        )
+        o_ref[...] = (accum / total).astype(o_ref.dtype)
+
+    return pl.pallas_call(
+        body,
+        grid=(rows // block,),
+        in_specs=[
+            pl.BlockSpec((block, depth), lambda i: (i, 0)),
+            pl.BlockSpec((keys, depth), lambda i: (0, 0)),
+            pl.BlockSpec((keys, depth), lambda i: (0, 0)),
+            pl.BlockSpec((1, keys), lambda i: (0, 0)),
+        ],
+        out_specs=pl.BlockSpec((block, depth), lambda i: (i, 0)),
+        out_shape=jax.ShapeDtypeStruct((rows, depth), query.dtype),
+        cost_estimate=pl.CostEstimate(
+            flops=4 * rows * keys * depth,
+            transcendentals=rows * keys,
+            bytes_accessed=2 * (2 * rows * depth + 2 * keys * depth) + 4 * keys,
+        ),
+    )(query, key, value, usable_row)
+
+
 def attend_by_head(
     queries, span_keys, span_values, cache_keys, cache_values, length, extra, companion
 ):
@@ -113,21 +158,14 @@
     owner = index // block_rows
     within = index % block_rows
     usable = (within < token_count) | (owner * cached_rows + within - token_count < length)
-    scores = (
-        jnp.einsum("thd,phd->htp", query_all, key_all, preferred_element_type=jnp.float32)
-        * scaling
-    )
-    scores = jnp.where(usable[None, None, :], scores, -1e30)
-    peak = jnp.max(scores, axis=2, keepdims=True)
-    weights = jnp.where(usable[None, None, :], jnp.exp(scores - peak), 0.0)
-    total = jnp.sum(weights, axis=2)
-    accum = jnp.einsum(
-        "htp,phd->thd",
-        weights.astype(jnp.bfloat16),
-        value_all,
-        preferred_element_type=jnp.float32,
-    )
-    head_out = (accum / total.T[:, :, None]).astype(jnp.bfloat16)
+    usable_row = usable.astype(jnp.int32)[None, :]
+    head_out = jnp.stack(
+        [
+            attend_one_head(query_all[:, h], key_all[:, h], value_all[:, h], usable_row)
+            for h in range(local_heads)
+        ],
+        1,
+    )
     head_out = head_out.reshape(ctx_count, token_count, width)
     back = lax.all_to_all(head_out, "ctx", split_axis=0, concat_axis=0, tiled=True)
     return back.transpose(1, 0, 2).reshape(token_count, column_count), extra_got, companion

time: 144 us -> 142 us (0.986)
  waiting for transfers between devices: 67.5 us -> 58.4 us
  Pallas kernels: 2.94 us -> 10.9 us
  matrix products: 23.9 us -> 19 us
  starting transfers between devices: 28.4 us -> 31.5 us
  local copies, waits for them, and re-layouts: 6.42 us -> 9.28 us
  other arithmetic: 11.4 us -> 9.19 us
    pallas_call x0 -> x1, Pallas kernels: none -> 7.96 us  [attend_one_head(): pl.pallas_call(body, grid=(rows // block,), in_specs=[pl.BlockSpec((block...]
    dot_general x2 -> x0, matrix products: 4.82 us -> none  [the longest x1 3 us: attend_by_head(): jnp.einsum('htp,phd->thd', weights.astype(jnp.bfloat16), value_all, prefe...]
    ppermute x20, waiting for transfers between devices: 37.2 us -> 32.4 us  [swap(): return lax.ppermute(rows, 'ctx', [(c, c ^ mask) for c in range(ctx_count)])]
    ppermute x2, waiting for transfers between devices: 22.6 us -> 18.9 us  [mover(): return lambda rows: lax.ppermute(rows, 'req', pairs)]
    ppermute x2, starting transfers between devices: 3.26 us -> 6.98 us  [mover(): return lambda rows: lax.ppermute(rows, 'req', pairs)]
    reduce_sum x1 -> x0, other arithmetic: 2.68 us -> none  [attend_by_head(): total = jnp.sum(weights, axis=2)]
    unnamed x23 -> x22, local copies, waits for them, and re-layouts: 0.92 us -> 2.86 us
  transfers between devices with their start and end apart: 24 -> 24, of which waited for: 19 -> 18; matrix products, arithmetic and copies ran while one was open for 10% -> 14% of each run, Pallas kernels for 0% -> 0%
where the time goes in v1:
time: 142 us; the launch traced here: 140 us
  waiting for transfers between devices  58.4 us (41%)
  starting transfers between devices  31.5 us (22%)
  matrix products  19 us (13%)
  Pallas kernels  10.9 us (8%)
  local copies, waits for them, and re-layouts  9.28 us (7%)
  other arithmetic  9.19 us (6%)
    ppermute x20, waiting for transfers between devices, swap(): return lax.ppermute(rows, 'ctx', [(c, c ^ mask) for c in range(ctx_count)])  32.4 us
    ppermute x2, waiting for transfers between devices, mover(): return lambda rows: lax.ppermute(rows, 'req', pairs)  18.9 us
    ppermute x20, starting transfers between devices, swap(): return lax.ppermute(rows, 'ctx', [(c, c ^ mask) for c in range(ctx_count)])  15.7 us
    pallas_call x1, Pallas kernels, attend_one_head(): pl.pallas_call(body, grid=(rows // block,), in_specs=[pl.BlockSpec((block...  7.96 us
    ppermute x2, starting transfers between devices, mover(): return lambda rows: lax.ppermute(rows, 'req', pairs)  6.98 us
    all_to_all x1, waiting for transfers between devices, attend_by_head(): lax.all_to_all(head_out, 'ctx', split_axis=0, concat_axis=0, tiled=True)  6.82 us
    dot_general x4, matrix products, experts_on(): up_val = jnp.dot(rows, up_proj[j], preferred_element_type=jnp.float32)  5.58 us
    dot_general x4, matrix products, experts_on(): jnp.dot(activated, down_proj[j], preferred_element_type=jnp.float32)  5.41 us
  transfers between devices with their start and end apart: 24, of which 18 were waited for; matrix products, arithmetic and copies ran while one was open for 14% of the time, Pallas kernels for 0%

profile of v1, /device:TPU:0, one launch (start us, length us, event | category | flops | bytes accessed | tf_op | source)
XLA Modules:
  0.0 139.9 jit_solution(5975895402013496115)
XLA Ops:
  1.4 2.9 %shard_map.271 = bf16[8,774,128]{2,1,0:T(8,128)(2,1)} custom-call(bf16[128,1024]{1,0:T(8,128)(2,1)} %refs_0_.1, bf16[128,1024]{1,0:T(8,128)(2,1)} %refs_1_.1, bf16[192,1024]{1,0:T(8,128)(2,1)} %refs_2_.1, bf16[128,1024]{1,0:T(8,128)(2,1)} %refs_3_.1, bf16[192,1024]{1,0:T(8,128)(2,1)} %refs_4_.1, bf16[8,6,128]{2,1,0:T(8,128)(2,1)} %copy.62.refs_5_), custom_call_target="tpu_custom_call" | custom-call | bytes 3170304 | tf_op jit(solution)/shard_map/pallas_call | solution.py:76
  4.3 5.3 %all-to-all-start = ((bf16[8,774,128]{2,1,0:T(8,128)(2,1)}), bf16[8,774,128]{2,1,0:T(8,128)(2,1)S(1)}, u32[]{:S(2)}, u32[]{:S(2)}) async-start(bf16[8,774,128]{2,1,0:T(8,128)(2,1)} %shard_map.271), calls=%async_computation | async-start | bytes 3178496 | tf_op jit(solution)/shard_map/all_to_all | solution.py:145
  11.0 16.3 %conditional.2 = (bf16[128,2048]{1,0:T(8,128)(2,1)S(1)}) conditional(s32[]{:T(128)} %clamp.6, bf16[128,2048]{1,0:T(8,128)(2,1)S(1)} %copy-done.1, bf16[128,2048]{1,0:T(8,128)(2,1)S(1)} %copy-done.1, bf16[128,2048]{1,0:T(8,128)(2,1)S(1)} %copy-done.1, bf16[128,2048]{1,0:T(8,128)(2,1)S(1)} %copy-done.1, ...), branch_computations={%region_3.4_spmd, %region_4.5_spmd, %region_5.6_spmd, %region_6.7_... | conditional | bytes 3145776 | solution.py:387
  11.1 3.5 %collective-permute-start.5 = (bf16[128,2048]{1,0:T(8,128)(2,1)S(1)}, bf16[128,2048]{1,0:T(8,128)(2,1)S(1)}, u32[]{:S(2)}, u32[]{:S(2)}) collective-permute-start(bf16[128,2048]{1,0:T(8,128)(2,1)S(1)} %param.6), channel_id=1, source_target_pairs={{0,8},{8,0},{16,16},{24,24},{1,9},{9,1},{17,17},{25,25},{2,10},{10... | collective-permute-start | bytes 1572872 | tf_op jit(solution)/shard_map/cond/branch_6_fun/ppermute | solution.py:385
  14.5 12.7 %collective-permute-done.5 = bf16[128,2048]{1,0:T(8,128)(2,1)S(1)} collective-permute-done((bf16[128,2048]{1,0:T(8,128)(2,1)S(1)}, bf16[128,2048]{1,0:T(8,128)(2,1)S(1)}, u32[]{:S(2)}, u32[]{:S(2)}) %collective-permute-start.5) | collective-permute-done | bytes 524320 | tf_op jit(solution)/shard_map/cond/branch_6_fun/ppermute | solution.py:385
  32.7 8.0 %shard_map.272 = bf16[1024,128]{1,0:T(8,128)(2,1)} custom-call(bf16[1024,128]{1,0:T(8,128)(2,1)} %bitcast.198, bf16[2560,128]{1,0:T(8,128)(2,1)} %bitcast.192, bf16[2560,128]{1,0:T(8,128)(2,1)} %bitcast.191, s32[1,2560]{1,0:T(1,128)} %or_convert_fusion.m_ref), custom_call_target="tpu_custom_call" | custom-call | flops 1342177280 | bytes 1845248 | tf_op jit(solution)/shard_map/pallas_call | solution.py:111
  40.7 3.6 %all-to-all-start.1 = ((bf16[8,128,128]{2,1,0:T(8,128)(2,1)}), bf16[8,128,128]{2,1,0:T(8,128)(2,1)S(1)}, u32[]{:S(2)}, u32[]{:S(2)}) async-start(bf16[8,128,128]{2,1,0:T(8,128)(2,1)} %bitcast.197), calls=%async_computation.1 | async-start | bytes 524288 | tf_op jit(solution)/shard_map/all_to_all | solution.py:170
  44.4 6.8 %all-to-all-done.1 = bf16[8,128,128]{2,1,0:T(8,128)(2,1)S(1)} async-done(((bf16[8,128,128]{2,1,0:T(8,128)(2,1)}), bf16[8,128,128]{2,1,0:T(8,128)(2,1)S(1)}, u32[]{:S(2)}, u32[]{:S(2)}) %all-to-all-start.1) | async-done | bytes 262176 | tf_op jit(solution)/shard_map/all_to_all | solution.py:170
  51.3 9.9 %conditional.3 = (bf16[134,1024]{1,0:T(8,128)(2,1)S(1)}) conditional(s32[]{:T(128)} %clamp.6, bf16[134,1024]{1,0:T(8,128)(2,1)S(1)} %pad_maximum_fusion.14, bf16[134,1024]{1,0:T(8,128)(2,1)S(1)} %pad_maximum_fusion.14, bf16[134,1024]{1,0:T(8,128)(2,1)S(1)} %pad_maximum_fusion.14, ...), branch_computations={%region_31.32_spmd, %region_32.33_spmd, %region_33.34_spmd, %regio... | conditional | bytes 1646640 | solution.py:387
  51.3 3.5 %collective-permute-start.28 = (bf16[134,1024]{1,0:T(8,128)(2,1)S(1)}, bf16[134,1024]{1,0:T(8,128)(2,1)S(1)}, u32[]{:S(2)}, u32[]{:S(2)}) collective-permute-start(bf16[134,1024]{1,0:T(8,128)(2,1)S(1)} %param.30), channel_id=1, source_target_pairs={{0,8},{8,0},{16,16},{24,24},{1,9},{9,1},{17,17},{25,25},{2,10},{10... | collective-permute-start | bytes 823304 | tf_op jit(solution)/shard_map/cond/branch_6_fun/ppermute | solution.py:385
  54.8 6.1 %collective-permute-done.28 = bf16[134,1024]{1,0:T(8,128)(2,1)S(1)} collective-permute-done((bf16[134,1024]{1,0:T(8,128)(2,1)S(1)}, bf16[134,1024]{1,0:T(8,128)(2,1)S(1)}, u32[]{:S(2)}, u32[]{:S(2)}) %collective-permute-start.28) | collective-permute-done | bytes 274464 | tf_op jit(solution)/shard_map/cond/branch_6_fun/ppermute | solution.py:385
  61.2 3.0 %multiply_reduce_fusion = (f32[128]{0:T(128)S(1)}, f32[128,2048]{1,0:T(8,128)S(1)}) fusion(bf16[1024,2048]{1,0:T(8,128)(2,1)} %param.79, bf16[134,1024]{1,0:T(8,128)(2,1)S(1)} %get-tuple-element.218, bf16[128,2048]{1,0:T(8,128)(2,1)S(1)} %get-tuple-element.217), kind=kOutput, calls=%fused_computation.68 | convolution fusion | flops 537919360 | bytes 6029824 | tf_op jit(solution)/shard_map/dot_general | solution.py:251
  64.5 1.4 collective-permute-start.47
  66.3 3.2 %collective-permute-done.47 = bf16[1,32,2048]{2,1,0:T(8,128)(2,1)S(1)} collective-permute-done((bf16[1,32,2048]{2,1,0:T(8,128)(2,1)S(1)}, bf16[1,32,2048]{2,1,0:T(8,128)(2,1)S(1)}, u32[]{:S(2)}, u32[]{:S(2)}) %collective-permute-start.47) | collective-permute-done | bytes 131104 | tf_op jit(solution)/shard_map/ppermute | solution.py:335
  74.9 2.4 %collective-permute-done.48 = bf16[2,32,2048]{2,1,0:T(8,128)(2,1)S(1)} collective-permute-done((bf16[2,32,2048]{2,1,0:T(8,128)(2,1)S(1)}, bf16[2,32,2048]{2,1,0:T(8,128)(2,1)S(1)}, u32[]{:S(2)}, u32[]{:S(2)}) %collective-permute-start.48) | collective-permute-done | bytes 262176 | tf_op jit(solution)/shard_map/ppermute | solution.py:335
  77.3 2.0 %collective-permute-done.49 = bf16[2,32,2048]{2,1,0:T(8,128)(2,1)S(1)} collective-permute-done((bf16[2,32,2048]{2,1,0:T(8,128)(2,1)S(1)}, bf16[2,32,2048]{2,1,0:T(8,128)(2,1)S(1)}, u32[]{:S(2)}, u32[]{:S(2)}) %collective-permute-start.49) | collective-permute-done | bytes 262176 | tf_op jit(solution)/shard_map/ppermute | solution.py:335
  80.7 2.6 %collective-permute-done.50 = bf16[2,4,32,2048]{3,2,1,0:T(8,128)(2,1)S(1)} collective-permute-done((bf16[2,4,32,2048]{3,2,1,0:T(8,128)(2,1)}, bf16[2,4,32,2048]{3,2,1,0:T(8,128)(2,1)S(1)}, u32[]{:S(2)}, u32[]{:S(2)}) %collective-permute-start.50) | collective-permute-done | bytes 1048608 | tf_op jit(solution)/shard_map/ppermute | solution.py:335
  83.6 2.0 %copy-done.7 = bf16[2,2048,512]{2,1,0:T(8,128)(2,1)S(1)} copy-done((bf16[2,2048,512]{2,1,0:T(8,128)(2,1)S(1)}, bf16[2,2048,512]{2,1,0:T(8,128)(2,1)}, u32[]{:S(2)}) %copy-start.7) | copy-done | bytes 4194328
  88.1 1.4 collective-permute-start.52
  91.3 1.4 fusion.53
  94.8 1.4 %fusion.74 = (bf16[512,2048]{1,0:T(8,128)(2,1)S(1)}, f32[512,2048]{1,0:T(8,128)S(1)}) fusion(bf16[512,512]{1,0:T(8,128)(2,1)S(1)} %fusion.47, bf16[2,512,2048]{2,1,0:T(8,128)(2,1)S(1)} %copy-done, f32[512]{0:T(512)S(1)} %bitcast.202, bf16[512,2048]{1,0:T(8,128)(2,1)S(1)} %convolution_convert_fusion.3, f32[512]{0:T(512)S(1)} %bitcast.201), kind=kOutput, calls=%fused_computation.158 | convolution fusion | flops 1081081856 | bytes 11014144 | tf_op jit(solution)/shard_map/dot_general | solution.py:264
  97.3 1.5 %collective-permute-start.54 = (bf16[2,32,2048]{2,1,0:T(8,128)(2,1)S(1)}, bf16[2,32,2048]{2,1,0:T(8,128)(2,1)S(1)}, u32[]{:S(2)}, u32[]{:S(2)}) collective-permute-start(bf16[2,32,2048]{2,1,0:T(8,128)(2,1)S(1)} %pad_maximum_fusion.18), channel_id=1, source_target_pairs={{0,4},{1,5},{2,6},{3,7},{4,0},{5,1},{6,2},{7,3},{8,12},{9,13},{10,... | collective-permute-start | bytes 786440 | tf_op jit(solution)/shard_map/ppermute | solution.py:335
  99.0 5.1 %collective-permute-done.53 = bf16[2,32,2048]{2,1,0:T(8,128)(2,1)S(1)} collective-permute-done((bf16[2,32,2048]{2,1,0:T(8,128)(2,1)S(1)}, bf16[2,32,2048]{2,1,0:T(8,128)(2,1)S(1)}, u32[]{:S(2)}, u32[]{:S(2)}) %collective-permute-start.53) | collective-permute-done | bytes 262176 | tf_op jit(solution)/shard_map/ppermute | solution.py:335
  105.8 2.1 %collective-permute-done.55 = bf16[2,4,32,2048]{3,2,1,0:T(8,128)(2,1)S(1)} collective-permute-done((bf16[2,4,32,2048]{3,2,1,0:T(8,128)(2,1)S(1)}, bf16[2,4,32,2048]{3,2,1,0:T(8,128)(2,1)S(1)}, u32[]{:S(2)}, u32[]{:S(2)}) %collective-permute-start.55) | collective-permute-done | bytes 1048608 | tf_op jit(solution)/shard_map/ppermute | solution.py:335
  111.0 1.4 %collective-permute-start.58 = (bf16[2,32,2048]{2,1,0:T(8,128)(2,1)S(1)}, bf16[2,32,2048]{2,1,0:T(8,128)(2,1)S(1)}, u32[]{:S(2)}, u32[]{:S(2)}) collective-permute-start(bf16[2,32,2048]{2,1,0:T(8,128)(2,1)S(1)} %slice.459), channel_id=1, source_target_pairs={{0,4},{1,5},{2,6},{3,7},{4,0},{5,1},{6,2},{7,3},{8,12},{9,13},{10,... | collective-permute-start | bytes 786440 | tf_op jit(solution)/shard_map/ppermute | solution.py:335
  115.1 1.6 %fusion.50 = bf16[512,512]{1,0:T(8,128)(2,1)S(1)} fusion(bf16[512,2048]{1,0:T(8,128)(2,1)S(1)} %pad_maximum_fusion, bf16[2,2048,512]{2,1,0:T(8,128)(2,1)S(1)} %copy-done.8, f32[512,512]{1,0:T(8,128)S(1)} %fusion.16), kind=kOutput, calls=%fused_computation.51 | convolution fusion | flops 1075314688 | bytes 5767168 | tf_op jit(solution)/shard_map/dot_general | solution.py:261
  117.9 1.4 %fusion.75 = (bf16[512,2048]{1,0:T(8,128)(2,1)S(1)}, f32[512,2048]{1,0:T(8,128)S(1)}) fusion(bf16[512,512]{1,0:T(8,128)(2,1)S(1)} %fusion.44, bf16[2,512,2048]{2,1,0:T(8,128)(2,1)S(1)} %copy-done, f32[512]{0:T(512)S(1)} %bitcast.200, bf16[512,2048]{1,0:T(8,128)(2,1)S(1)} %convolution_convert_fusion.1, f32[512]{0:T(512)S(1)} %bitcast.199), kind=kOutput, calls=%fused_computation.159 | convolution fusion | flops 1081081856 | bytes 11014144 | tf_op jit(solution)/shard_map/dot_general | solution.py:264
  120.6 1.4 collective-permute-start.60
  122.8 1.7 %collective-permute-start.63 = (bf16[2,32,2048]{2,1,0:T(8,128)(2,1)S(1)}, bf16[2,32,2048]{2,1,0:T(8,128)(2,1)S(1)}, u32[]{:S(2)}, u32[]{:S(2)}) collective-permute-start(bf16[2,32,2048]{2,1,0:T(8,128)(2,1)S(1)} %slice.457), channel_id=1, source_target_pairs={{0,4},{1,5},{2,6},{3,7},{4,0},{5,1},{6,2},{7,3},{8,12},{9,13},{10,... | collective-permute-start | bytes 786440 | tf_op jit(solution)/shard_map/ppermute | solution.py:335
  124.4 1.5 %collective-permute-done.60 = bf16[1,32,2048]{2,1,0:T(8,128)(2,1)S(1)} collective-permute-done((bf16[1,32,2048]{2,1,0:T(8,128)(2,1)S(1)}, bf16[1,32,2048]{2,1,0:T(8,128)(2,1)S(1)}, u32[]{:S(2)}, u32[]{:S(2)}) %collective-permute-start.60) | collective-permute-done | bytes 131104 | tf_op jit(solution)/shard_map/ppermute | solution.py:335
  127.1 5.4 %collective-permute-done.63 = bf16[2,32,2048]{2,1,0:T(8,128)(2,1)S(1)} collective-permute-done((bf16[2,32,2048]{2,1,0:T(8,128)(2,1)S(1)}, bf16[2,32,2048]{2,1,0:T(8,128)(2,1)S(1)}, u32[]{:S(2)}, u32[]{:S(2)}) %collective-permute-start.63) | collective-permute-done | bytes 262176 | tf_op jit(solution)/shard_map/ppermute | solution.py:335
  134.4 4.1 %collective-permute-done.65 = bf16[1,32,2048]{2,1,0:T(8,128)(2,1)S(1)} collective-permute-done((bf16[1,32,2048]{2,1,0:T(8,128)(2,1)S(1)}, bf16[1,32,2048]{2,1,0:T(8,128)(2,1)S(1)}, u32[]{:S(2)}, u32[]{:S(2)}) %collective-permute-start.65) | collective-permute-done | bytes 131104 | tf_op jit(solution)/shard_map/ppermute | solution.py:335
  (141 shorter events, 37.9 us)
Async XLA Ops:
  4.3 5.3 %copy-start.3 = (s32[24,4]{0,1:T(4,128)S(1)}, s32[24,4]{0,1:T(4,128)}, u32[]{:S(2)}) copy-start(s32[24,4]{0,1:T(4,128)} %constant.68.clone) | copy-start | bytes 1156
  4.3 5.3 %copy-start.6 = (s32[4]{0:T(128)S(1)}, s32[4]{0:T(128)}, u32[]{:S(2)}) copy-start(s32[4]{0:T(128)} %param.78) | copy-start | bytes 52
  4.3 6.1 %copy-start.1 = (bf16[128,2048]{1,0:T(8,128)(2,1)S(1)}, bf16[128,2048]{1,0:T(8,128)(2,1)}, u32[]{:S(2)}) copy-start(bf16[128,2048]{1,0:T(8,128)(2,1)} %param.71) | copy-start | bytes 1572868
  4.3 26.5 %all-to-all-start = ((bf16[8,774,128]{2,1,0:T(8,128)(2,1)}), bf16[8,774,128]{2,1,0:T(8,128)(2,1)S(1)}, u32[]{:S(2)}, u32[]{:S(2)}) async-start(bf16[8,774,128]{2,1,0:T(8,128)(2,1)} %shard_map.271), calls=%async_computation | async-start | bytes 3178496 | tf_op jit(solution)/shard_map/all_to_all | solution.py:145
  11.0 17.0 %copy-start.9 = (s32[4]{0:T(128)S(1)}, s32[4]{0:T(128)}, u32[]{:S(2)}) copy-start(s32[4]{0:T(128)} %param.77) | copy-start | bytes 52
  11.1 16.2 %collective-permute-start.5 = (bf16[128,2048]{1,0:T(8,128)(2,1)S(1)}, bf16[128,2048]{1,0:T(8,128)(2,1)S(1)}, u32[]{:S(2)}, u32[]{:S(2)}) collective-permute-start(bf16[128,2048]{1,0:T(8,128)(2,1)S(1)} %param.6), channel_id=1, source_target_pairs={{0,8},{8,0},{16,16},{24,24},{1,9},{9,1},{17,17},{25,25},{2,10},{10... | collective-permute-start | bytes 1572872 | tf_op jit(solution)/shard_map/cond/branch_6_fun/ppermute | solution.py:385
  32.7 11.5 %copy-start.4 = (s32[8]{0:T(128)S(1)}, s32[8]{0:T(128)}, u32[]{:S(2)}) copy-start(s32[8]{0:T(128)} %constant.70.clone) | copy-start | bytes 100
  32.7 11.5 %copy-start.5 = (s32[8]{0:T(128)S(1)}, s32[8]{0:T(128)}, u32[]{:S(2)}) copy-start(s32[8]{0:T(128)} %constant.69.clone) | copy-start | bytes 100
  40.7 10.5 %all-to-all-start.1 = ((bf16[8,128,128]{2,1,0:T(8,128)(2,1)}), bf16[8,128,128]{2,1,0:T(8,128)(2,1)S(1)}, u32[]{:S(2)}, u32[]{:S(2)}) async-start(bf16[8,128,128]{2,1,0:T(8,128)(2,1)} %bitcast.197), calls=%async_computation.1 | async-start | bytes 524288 | tf_op jit(solution)/shard_map/all_to_all | solution.py:170
  51.3 9.6 %collective-permute-start.28 = (bf16[134,1024]{1,0:T(8,128)(2,1)S(1)}, bf16[134,1024]{1,0:T(8,128)(2,1)S(1)}, u32[]{:S(2)}, u32[]{:S(2)}) collective-permute-start(bf16[134,1024]{1,0:T(8,128)(2,1)S(1)} %param.30), channel_id=1, source_target_pairs={{0,8},{8,0},{16,16},{24,24},{1,9},{9,1},{17,17},{25,25},{2,10},{10... | collective-permute-start | bytes 823304 | tf_op jit(solution)/shard_map/cond/branch_6_fun/ppermute | solution.py:385
  61.2 3.1 %copy-start.2 = (f32[2048]{0:T(1024)S(1)}, f32[2048]{0:T(1024)}, u32[]{:S(2)}) copy-start(f32[2048]{0:T(1024)} %param.80) | copy-start | bytes 24580
  64.5 5.0 %collective-permute-start.47 = (bf16[1,32,2048]{2,1,0:T(8,128)(2,1)S(1)}, bf16[1,32,2048]{2,1,0:T(8,128)(2,1)S(1)}, u32[]{:S(2)}, u32[]{:S(2)}) collective-permute-start(bf16[1,32,2048]{2,1,0:T(8,128)(2,1)S(1)} %get-tuple-element.188), channel_id=1, source_target_pairs={{0,2},{1,3},{2,0},{3,1},{4,6},{5,7},{6,4},{7,5},{8,10},{9,11},{10,... | collective-permute-start | bytes 393224 | tf_op jit(solution)/shard_map/ppermute | solution.py:335
  65.9 5.0 %collective-permute-start.46 = (bf16[1,32,2048]{2,1,0:T(8,128)(2,1)S(1)}, bf16[1,32,2048]{2,1,0:T(8,128)(2,1)S(1)}, u32[]{:S(2)}, u32[]{:S(2)}) collective-permute-start(bf16[1,32,2048]{2,1,0:T(8,128)(2,1)S(1)} %get-tuple-element.189), channel_id=1, source_target_pairs={{0,4},{1,5},{2,6},{3,7},{4,0},{5,1},{6,2},{7,3},{8,12},{9,13},{10,... | collective-permute-start | bytes 393224 | tf_op jit(solution)/shard_map/ppermute | solution.py:335
  70.9 6.4 %collective-permute-start.48 = (bf16[2,32,2048]{2,1,0:T(8,128)(2,1)S(1)}, bf16[2,32,2048]{2,1,0:T(8,128)(2,1)S(1)}, u32[]{:S(2)}, u32[]{:S(2)}) collective-permute-start(bf16[2,32,2048]{2,1,0:T(8,128)(2,1)S(1)} %pad_maximum_fusion.15), channel_id=1, source_target_pairs={{0,2},{1,3},{2,0},{3,1},{4,6},{5,7},{6,4},{7,5},{8,10},{9,11},{10,... | collective-permute-start | bytes 786440 | tf_op jit(solution)/shard_map/ppermute | solution.py:335
  72.9 6.4 %collective-permute-start.49 = (bf16[2,32,2048]{2,1,0:T(8,128)(2,1)S(1)}, bf16[2,32,2048]{2,1,0:T(8,128)(2,1)S(1)}, u32[]{:S(2)}, u32[]{:S(2)}) collective-permute-start(bf16[2,32,2048]{2,1,0:T(8,128)(2,1)S(1)} %pad_maximum_fusion.16), channel_id=1, source_target_pairs={{0,4},{1,5},{2,6},{3,7},{4,0},{5,1},{6,2},{7,3},{8,12},{9,13},{10,... | collective-permute-start | bytes 786440 | tf_op jit(solution)/shard_map/ppermute | solution.py:335
  80.4 2.9 %collective-permute-start.50 = (bf16[2,4,32,2048]{3,2,1,0:T(8,128)(2,1)}, bf16[2,4,32,2048]{3,2,1,0:T(8,128)(2,1)S(1)}, u32[]{:S(2)}, u32[]{:S(2)}) collective-permute-start(bf16[2,4,32,2048]{3,2,1,0:T(8,128)(2,1)} %pad_maximum_fusion.2), channel_id=1, source_target_pairs={{0,1},{1,0},{2,3},{3,2},{4,5},{5,4},{6,7},{7,6},{8,9},{9,8},{10,11... | collective-permute-start | bytes 3145736 | tf_op jit(solution)/shard_map/ppermute | solution.py:335
  86.8 3.1 %copy-start.8 = (bf16[2,2048,512]{2,1,0:T(8,128)(2,1)S(1)}, bf16[2,2048,512]{2,1,0:T(8,128)(2,1)}, u32[]{:S(2)}) copy-start(bf16[2,2048,512]{2,1,0:T(8,128)(2,1)} %param.84) | copy-start | bytes 12582916
  88.1 8.1 %collective-permute-start.52 = (bf16[1,32,2048]{2,1,0:T(8,128)(2,1)S(1)}, bf16[1,32,2048]{2,1,0:T(8,128)(2,1)S(1)}, u32[]{:S(2)}, u32[]{:S(2)}) collective-permute-start(bf16[1,32,2048]{2,1,0:T(8,128)(2,1)S(1)} %bitcast.195), channel_id=1, source_target_pairs={{0,2},{1,3},{2,0},{3,1},{4,6},{5,7},{6,4},{7,5},{8,10},{9,11},{10,... | collective-permute-start | bytes 393224 | tf_op jit(solution)/shard_map/ppermute | solution.py:335
  89.5 6.8 %collective-permute-start.51 = (bf16[1,32,2048]{2,1,0:T(8,128)(2,1)S(1)}, bf16[1,32,2048]{2,1,0:T(8,128)(2,1)S(1)}, u32[]{:S(2)}, u32[]{:S(2)}) collective-permute-start(bf16[1,32,2048]{2,1,0:T(8,128)(2,1)S(1)} %bitcast.193), channel_id=1, source_target_pairs={{0,4},{1,5},{2,6},{3,7},{4,0},{5,1},{6,2},{7,3},{8,12},{9,13},{10,... | collective-permute-start | bytes 393224 | tf_op jit(solution)/shard_map/ppermute | solution.py:335
  96.3 7.9 %collective-permute-start.53 = (bf16[2,32,2048]{2,1,0:T(8,128)(2,1)S(1)}, bf16[2,32,2048]{2,1,0:T(8,128)(2,1)S(1)}, u32[]{:S(2)}, u32[]{:S(2)}) collective-permute-start(bf16[2,32,2048]{2,1,0:T(8,128)(2,1)S(1)} %pad_maximum_fusion.17), channel_id=1, source_target_pairs={{0,2},{1,3},{2,0},{3,1},{4,6},{5,7},{6,4},{7,5},{8,10},{9,11},{10,... | collective-permute-start | bytes 786440 | tf_op jit(solution)/shard_map/ppermute | solution.py:335
  97.3 7.7 %collective-permute-start.54 = (bf16[2,32,2048]{2,1,0:T(8,128)(2,1)S(1)}, bf16[2,32,2048]{2,1,0:T(8,128)(2,1)S(1)}, u32[]{:S(2)}, u32[]{:S(2)}) collective-permute-start(bf16[2,32,2048]{2,1,0:T(8,128)(2,1)S(1)} %pad_maximum_fusion.18), channel_id=1, source_target_pairs={{0,4},{1,5},{2,6},{3,7},{4,0},{5,1},{6,2},{7,3},{8,12},{9,13},{10,... | collective-permute-start | bytes 786440 | tf_op jit(solution)/shard_map/ppermute | solution.py:335
  98.9 6.5 %collective-permute-start.56 = (bf16[2,4,32,2048]{3,2,1,0:T(8,128)(2,1)S(1)}, bf16[2,4,32,2048]{3,2,1,0:T(8,128)(2,1)S(1)}, u32[]{:S(2)}, u32[]{:S(2)}) collective-permute-start(bf16[2,4,32,2048]{3,2,1,0:T(8,128)(2,1)S(1)} %pad_maximum_fusion.8), channel_id=1, source_target_pairs={{0,1},{1,0},{2,3},{3,2},{4,5},{5,4},{6,7},{7,6},{8,9},{9,8},{10,11... | collective-permute-start | bytes 3145736 | tf_op jit(solution)/shard_map/ppermute | solution.py:335
  105.2 2.7 %collective-permute-start.55 = (bf16[2,4,32,2048]{3,2,1,0:T(8,128)(2,1)S(1)}, bf16[2,4,32,2048]{3,2,1,0:T(8,128)(2,1)S(1)}, u32[]{:S(2)}, u32[]{:S(2)}) collective-permute-start(bf16[2,4,32,2048]{3,2,1,0:T(8,128)(2,1)S(1)} %pad_maximum_fusion.5), channel_id=1, source_target_pairs={{0,1},{1,0},{2,3},{3,2},{4,5},{5,4},{6,7},{7,6},{8,9},{9,8},{10,11... | collective-permute-start | bytes 3145736 | tf_op jit(solution)/shard_map/ppermute | solution.py:335
  111.0 8.9 %collective-permute-start.58 = (bf16[2,32,2048]{2,1,0:T(8,128)(2,1)S(1)}, bf16[2,32,2048]{2,1,0:T(8,128)(2,1)S(1)}, u32[]{:S(2)}, u32[]{:S(2)}) collective-permute-start(bf16[2,32,2048]{2,1,0:T(8,128)(2,1)S(1)} %slice.459), channel_id=1, source_target_pairs={{0,4},{1,5},{2,6},{3,7},{4,0},{5,1},{6,2},{7,3},{8,12},{9,13},{10,... | collective-permute-start | bytes 786440 | tf_op jit(solution)/shard_map/ppermute | solution.py:335
  112.4 8.1 %collective-permute-start.57 = (bf16[2,32,2048]{2,1,0:T(8,128)(2,1)S(1)}, bf16[2,32,2048]{2,1,0:T(8,128)(2,1)S(1)}, u32[]{:S(2)}, u32[]{:S(2)}) collective-permute-start(bf16[2,32,2048]{2,1,0:T(8,128)(2,1)S(1)} %slice.460), channel_id=1, source_target_pairs={{0,2},{1,3},{2,0},{3,1},{4,6},{5,7},{6,4},{7,5},{8,10},{9,11},{10,... | collective-permute-start | bytes 786440 | tf_op jit(solution)/shard_map/ppermute | solution.py:335
  119.5 2.8 %collective-permute-start.61 = (bf16[2,4,32,2048]{3,2,1,0:T(8,128)(2,1)S(1)}, bf16[2,4,32,2048]{3,2,1,0:T(8,128)(2,1)S(1)}, u32[]{:S(2)}, u32[]{:S(2)}) collective-permute-start(bf16[2,4,32,2048]{3,2,1,0:T(8,128)(2,1)S(1)} %pad_maximum_fusion.9), channel_id=1, source_target_pairs={{0,1},{1,0},{2,3},{3,2},{4,5},{5,4},{6,7},{7,6},{8,9},{9,8},{10,11... | collective-permute-start | bytes 3145736 | tf_op jit(solution)/shard_map/ppermute | solution.py:335
  120.6 5.4 %collective-permute-start.60 = (bf16[1,32,2048]{2,1,0:T(8,128)(2,1)S(1)}, bf16[1,32,2048]{2,1,0:T(8,128)(2,1)S(1)}, u32[]{:S(2)}, u32[]{:S(2)}) collective-permute-start(bf16[1,32,2048]{2,1,0:T(8,128)(2,1)S(1)} %slice.463), channel_id=1, source_target_pairs={{0,2},{1,3},{2,0},{3,1},{4,6},{5,7},{6,4},{7,5},{8,10},{9,11},{10,... | collective-permute-start | bytes 393224 | tf_op jit(solution)/shard_map/ppermute | solution.py:335
  122.0 11.9 %collective-permute-start.59 = (bf16[1,32,2048]{2,1,0:T(8,128)(2,1)S(1)}, bf16[1,32,2048]{2,1,0:T(8,128)(2,1)S(1)}, u32[]{:S(2)}, u32[]{:S(2)}) collective-permute-start(bf16[1,32,2048]{2,1,0:T(8,128)(2,1)S(1)} %slice.464), channel_id=1, source_target_pairs={{0,4},{1,5},{2,6},{3,7},{4,0},{5,1},{6,2},{7,3},{8,12},{9,13},{10,... | collective-permute-start | bytes 393224 | tf_op jit(solution)/shard_map/ppermute | solution.py:335
  122.8 9.7 %collective-permute-start.63 = (bf16[2,32,2048]{2,1,0:T(8,128)(2,1)S(1)}, bf16[2,32,2048]{2,1,0:T(8,128)(2,1)S(1)}, u32[]{:S(2)}, u32[]{:S(2)}) collective-permute-start(bf16[2,32,2048]{2,1,0:T(8,128)(2,1)S(1)} %slice.457), channel_id=1, source_target_pairs={{0,4},{1,5},{2,6},{3,7},{4,0},{5,1},{6,2},{7,3},{8,12},{9,13},{10,... | collective-permute-start | bytes 786440 | tf_op jit(solution)/shard_map/ppermute | solution.py:335
  126.1 7.4 %collective-permute-start.62 = (bf16[2,32,2048]{2,1,0:T(8,128)(2,1)S(1)}, bf16[2,32,2048]{2,1,0:T(8,128)(2,1)S(1)}, u32[]{:S(2)}, u32[]{:S(2)}) collective-permute-start(bf16[2,32,2048]{2,1,0:T(8,128)(2,1)S(1)} %slice.458), channel_id=1, source_target_pairs={{0,2},{1,3},{2,0},{3,1},{4,6},{5,7},{6,4},{7,5},{8,10},{9,11},{10,... | collective-permute-start | bytes 786440 | tf_op jit(solution)/shard_map/ppermute | solution.py:335
  133.5 5.0 %collective-permute-start.65 = (bf16[1,32,2048]{2,1,0:T(8,128)(2,1)S(1)}, bf16[1,32,2048]{2,1,0:T(8,128)(2,1)S(1)}, u32[]{:S(2)}, u32[]{:S(2)}) collective-permute-start(bf16[1,32,2048]{2,1,0:T(8,128)(2,1)S(1)} %slice.461), channel_id=1, source_target_pairs={{0,2},{1,3},{2,0},{3,1},{4,6},{5,7},{6,4},{7,5},{8,10},{9,11},{10,... | collective-permute-start | bytes 393224 | tf_op jit(solution)/shard_map/ppermute | solution.py:335
  133.9 5.0 %collective-permute-start.64 = (bf16[1,32,2048]{2,1,0:T(8,128)(2,1)S(1)}, bf16[1,32,2048]{2,1,0:T(8,128)(2,1)S(1)}, u32[]{:S(2)}, u32[]{:S(2)}) collective-permute-start(bf16[1,32,2048]{2,1,0:T(8,128)(2,1)S(1)} %slice.462), channel_id=1, source_target_pairs={{0,4},{1,5},{2,6},{3,7},{4,0},{5,1},{6,2},{7,3},{8,12},{9,13},{10,... | collective-permute-start | bytes 393224 | tf_op jit(solution)/shard_map/ppermute | solution.py:335
  (2 other events, 4.4 us)

commit v2 on v0

--- a/solution.py
+++ b/solution.py
@@ -232,37 +232,34 @@
 
     if ctx_count & (ctx_count - 1) == 0 and ctx_count > 1 and token_count % 4 == 0:
         me = lax.axis_index("ctx")
-        stream_rows = token_count // 4
+        stream_rows = token_count // 2
         orders = xor_orders(ctx_count)
-        moe_pieces = []
-        earlier = None
-        pending = None
         steps = len(orders[0])
-        for group in range(2):
-            firsts = [(2 * group + s) * stream_rows for s in range(2)]
-            inputs = [normed[f : f + stream_rows] for f in firsts]
-            if earlier is not None:
-                inputs, _ = lax.optimization_barrier((inputs, earlier))
-            helds = gather_xor(inputs, orders, ctx_count)
-            earlier = helds
-            gates = []
-            for first, order in zip(firsts, orders):
-                sources = jnp.array(relative_masks(order), jnp.int32) ^ me
-                gates.append(
-                    jnp.take(
-                        local_gates[:, :, first : first + stream_rows], sources, axis=1
-                    ).reshape(local_experts, ctx_count * stream_rows)
-                )
-            rows = jnp.concatenate(
-                [held.reshape(ctx_count * stream_rows, feature_width) for held in helds], 0
-            )
-            if pending is not None:
-                rows, pending = lax.optimization_barrier((rows, pending))
-                moe_pieces.extend(reduce_xor(pending, orders, ctx_count, steps - 1))
-            part = experts_on(rows, jnp.concatenate(gates, 1))
-            part = part.reshape(2, ctx_count, stream_rows, feature_width)
-            pending = reduce_xor([part[0], part[1]], orders, ctx_count, steps, steps - 1)
-        moe_pieces.extend(reduce_xor(pending, orders, ctx_count, steps - 1))
+        firsts = [s * stream_rows for s in range(2)]
+        inputs = [normed[f : f + stream_rows] for f in firsts]
+        helds = gather_xor(inputs, [order[:-1] for order in orders], ctx_count)
+        last_mask = 1 << orders[0][-1]
+        arrived = swap(jnp.stack(helds), last_mask, ctx_count)
+        half_blocks = ctx_count // 2
+        gates_own, gates_arrived = [], []
+        for first, order in zip(firsts, orders):
+            sources = jnp.array(relative_masks(order), jnp.int32) ^ me
+            gates = jnp.take(local_gates[:, :, first : first + stream_rows], sources, axis=1)
+            gates_own.append(gates[:, :half_blocks].reshape(local_experts, -1))
+            gates_arrived.append(gates[:, half_blocks:].reshape(local_experts, -1))
+        half_rows = half_blocks * stream_rows
+        own_part = experts_on(
+            jnp.concatenate([held.reshape(half_rows, feature_width) for held in helds], 0),
+            jnp.concatenate(gates_own, 1),
+        )
+        arrived_part = experts_on(
+            arrived.reshape(2 * half_rows, feature_width), jnp.concatenate(gates_arrived, 1)
+        )
+        returned = swap(arrived_part.astype(jnp.bfloat16), last_mask, ctx_count)
+        totals = own_part + returned.astype(jnp.float32)
+        totals = totals.reshape(2, half_blocks, stream_rows, feature_width)
+        totals = list(lax.optimization_barrier((totals[0], totals[1])))
+        moe_pieces = reduce_xor(totals, orders, ctx_count, steps - 1)
         moe_rows = jnp.concatenate(moe_pieces, 0)
     else:
         normed_all = lax.all_gather(normed, "ctx", axis=0, tiled=True)

time: 144 us -> 141 us (0.979)
  the two profiles are of different devices: /device:TPU:0 before, /device:TPU:16 now
where the time goes in v2:
time: 141 us; the launch traced here: 139 us
  waiting for transfers between devices  64.4 us (46%)
  matrix products  31.3 us (22%)
  starting transfers between devices  22.4 us (16%)
  other arithmetic  12.4 us (9%)
  local copies, waits for them, and re-layouts  4.19 us (3%)
  Pallas kernels  2.98 us (2%)
    ppermute x10, waiting for transfers between devices, swap(): return lax.ppermute(rows, 'ctx', [(c, c ^ mask) for c in range(ctx_count)])  35.6 us
    ppermute x2, waiting for transfers between devices, mover(): return lambda rows: lax.ppermute(rows, 'req', pairs)  21.1 us
    ppermute x10, starting transfers between devices, swap(): return lax.ppermute(rows, 'ctx', [(c, c ^ mask) for c in range(ctx_count)])  10.6 us
    dot_general x4, matrix products, experts_on(): gate_val = jnp.dot(rows, gate_proj[j], preferred_element_type=jnp.float32)  8.99 us
    dot_general x4, matrix products, experts_on(): up_val = jnp.dot(rows, up_proj[j], preferred_element_type=jnp.float32)  8.74 us
    all_to_all x1, waiting for transfers between devices, attend_by_head(): lax.all_to_all(head_out, 'ctx', split_axis=0, concat_axis=0, tiled=True)  6.82 us
    dot_general x4, matrix products, experts_on(): jnp.dot(activated, down_proj[j], preferred_element_type=jnp.float32)  5.74 us
    ppermute x2, starting transfers between devices, mover(): return lambda rows: lax.ppermute(rows, 'req', pairs)  4.71 us
  transfers between devices with their start and end apart: 14, of which 13 were waited for; matrix products, arithmetic and copies ran while one was open for 9% of the time, Pallas kernels for 0%

profile of v2, /device:TPU:16, one launch (start us, length us, event | category | flops | bytes accessed | tf_op | source)
XLA Modules:
  0.0 139.3 jit_solution(12507205465937571757)
XLA Ops:
  1.4 3.0 %shard_map.253 = bf16[8,774,128]{2,1,0:T(8,128)(2,1)} custom-call(bf16[128,1024]{1,0:T(8,128)(2,1)} %refs_0_.1, bf16[128,1024]{1,0:T(8,128)(2,1)} %refs_1_.1, bf16[192,1024]{1,0:T(8,128)(2,1)} %refs_2_.1, bf16[128,1024]{1,0:T(8,128)(2,1)} %refs_3_.1, bf16[192,1024]{1,0:T(8,128)(2,1)} %refs_4_.1, bf16[8,6,128]{2,1,0:T(8,128)(2,1)} %copy.74.refs_5_), custom_call_target="tpu_custom_call" | custom-call | bytes 3170304 | tf_op jit(solution)/shard_map/pallas_call | solution.py:76
  4.4 3.7 %all-to-all-start = ((bf16[8,774,128]{2,1,0:T(8,128)(2,1)}), bf16[8,774,128]{2,1,0:T(8,128)(2,1)S(1)}, u32[]{:S(2)}, u32[]{:S(2)}) async-start(bf16[8,774,128]{2,1,0:T(8,128)(2,1)} %shard_map.253), calls=%async_computation | async-start | bytes 3178496 | tf_op jit(solution)/shard_map/all_to_all | solution.py:100
  9.5 16.3 %conditional.2 = (bf16[128,2048]{1,0:T(8,128)(2,1)S(1)}) conditional(s32[]{:T(128)} %clamp.6, bf16[128,2048]{1,0:T(8,128)(2,1)S(1)} %copy-done, bf16[128,2048]{1,0:T(8,128)(2,1)S(1)} %copy-done, bf16[128,2048]{1,0:T(8,128)(2,1)S(1)} %copy-done, bf16[128,2048]{1,0:T(8,128)(2,1)S(1)} %copy-done, ...), branch_computations={%region_3.4_spmd, %region_4.5_spmd, %region_5.6_spmd, %region_6.7_... | conditional | bytes 3145776 | solution.py:346
  9.6 2.4 %collective-permute-start.1 = (bf16[128,2048]{1,0:T(8,128)(2,1)S(1)}, bf16[128,2048]{1,0:T(8,128)(2,1)S(1)}, u32[]{:S(2)}, u32[]{:S(2)}) collective-permute-start(bf16[128,2048]{1,0:T(8,128)(2,1)S(1)} %param.2), channel_id=1, source_target_pairs={{0,0},{8,16},{16,8},{24,24},{1,1},{9,17},{17,9},{25,25},{2,2},{10,... | collective-permute-start | bytes 1572872 | tf_op jit(solution)/shard_map/cond/branch_2_fun/ppermute | solution.py:344
  12.0 13.9 %collective-permute-done.1 = bf16[128,2048]{1,0:T(8,128)(2,1)S(1)} collective-permute-done((bf16[128,2048]{1,0:T(8,128)(2,1)S(1)}, bf16[128,2048]{1,0:T(8,128)(2,1)S(1)}, u32[]{:S(2)}, u32[]{:S(2)}) %collective-permute-start.1) | collective-permute-done | bytes 524320 | tf_op jit(solution)/shard_map/cond/branch_2_fun/ppermute | solution.py:344
  29.5 1.8 %fusion = (f32[1024]{0:T(1024)S(1)}, f32[1024,2560]{1,0:T(8,128)S(1)}) fusion(pred[2560]{0:T(1024)(128)(4,1)S(1)} %fusion.74, bf16[1024,128]{1,0:T(8,128)(2,1)S(1)} %bitcast.143, bf16[2560,128]{1,0:T(8,128)(2,1)S(1)} %bitcast.140), kind=kOutput, calls=%fused_computation.4 | convolution fusion | flops 678951936 | bytes 11409920 | tf_op jit(solution)/shard_map/thd,phd->htp/dot_general | solution.py:117
  31.3 2.7 %fusion.1 = f32[1024]{0:T(1024)S(1)} fusion(f32[1024,2560]{1,0:T(8,128)S(1)} %get-tuple-element.152, f32[1024]{0:T(1024)S(1)} %get-tuple-element.151, pred[2560]{0:T(1024)(128)(4,1)S(1)} %fusion.74), kind=kLoop, calls=%fused_computation.5 | loop fusion | flops 13106176 | bytes 10496512 | tf_op jit(solution)/shard_map/reduce_sum | solution.py:123
  34.0 3.0 %fusion.60 = bf16[16,8,8,128]{3,1,2,0:T(8,128)(2,1)S(1)} fusion(bf16[2560,128]{1,0:T(8,128)(2,1)S(1)} %bitcast.146, f32[1024,2560]{1,0:T(8,128)S(1)} %get-tuple-element.152, f32[1024]{0:T(1024)S(1)} %get-tuple-element.151, pred[2560]{0:T(1024)(128)(4,1)S(1)} %fusion.74, f32[1024]{0:T(1024)S(1)} %fusion.1), kind=kOutput, calls=%fused_computation.69 | convolution fusion | flops 684457984 | bytes 11414016 | tf_op jit(solution)/shard_map/htp,phd->thd/dot_general | solution.py:124
  37.8 3.4 %all-to-all-start.1 = ((bf16[8,128,128]{1,2,0:T(8,128)(2,1)}), bf16[8,128,128]{1,2,0:T(8,128)(2,1)S(1)}, u32[]{:S(2)}, u32[]{:S(2)}) async-start(bf16[8,128,128]{1,2,0:T(8,128)(2,1)} %copy.75), calls=%async_computation.1 | async-start | bytes 524288 | tf_op jit(solution)/shard_map/all_to_all | solution.py:132
  41.3 6.8 %all-to-all-done.1 = bf16[8,128,128]{1,2,0:T(8,128)(2,1)S(1)} async-done(((bf16[8,128,128]{1,2,0:T(8,128)(2,1)}), bf16[8,128,128]{1,2,0:T(8,128)(2,1)S(1)}, u32[]{:S(2)}, u32[]{:S(2)}) %all-to-all-start.1) | async-done | bytes 262176 | tf_op jit(solution)/shard_map/all_to_all | solution.py:132
  48.3 9.9 %conditional.3 = (bf16[134,1024]{1,0:T(8,128)(2,1)S(1)}) conditional(s32[]{:T(128)} %clamp.6, bf16[134,1024]{1,0:T(8,128)(2,1)S(1)} %pad_maximum_fusion.6, bf16[134,1024]{1,0:T(8,128)(2,1)S(1)} %pad_maximum_fusion.6, bf16[134,1024]{1,0:T(8,128)(2,1)S(1)} %pad_maximum_fusion.6, ...), branch_computations={%region_33.34_spmd, %region_34.35_spmd, %region_35.36_spmd, %regio... | conditional | bytes 1646640 | solution.py:346
  48.3 2.4 %collective-permute-start.24 = (bf16[134,1024]{1,0:T(8,128)(2,1)S(1)}, bf16[134,1024]{1,0:T(8,128)(2,1)S(1)}, u32[]{:S(2)}, u32[]{:S(2)}) collective-permute-start(bf16[134,1024]{1,0:T(8,128)(2,1)S(1)} %param.26), channel_id=1, source_target_pairs={{0,0},{8,16},{16,8},{24,24},{1,1},{9,17},{17,9},{25,25},{2,2},{10,... | collective-permute-start | bytes 823304 | tf_op jit(solution)/shard_map/cond/branch_2_fun/ppermute | solution.py:344
  50.7 7.3 %collective-permute-done.24 = bf16[134,1024]{1,0:T(8,128)(2,1)S(1)} collective-permute-done((bf16[134,1024]{1,0:T(8,128)(2,1)S(1)}, bf16[134,1024]{1,0:T(8,128)(2,1)S(1)}, u32[]{:S(2)}, u32[]{:S(2)}) %collective-permute-start.24) | collective-permute-done | bytes 274464 | tf_op jit(solution)/shard_map/cond/branch_2_fun/ppermute | solution.py:344
  58.2 3.0 %multiply_reduce_fusion = (f32[128]{0:T(128)S(1)}, f32[128,2048]{1,0:T(8,128)S(1)}) fusion(bf16[1024,2048]{1,0:T(8,128)(2,1)} %param.77, bf16[134,1024]{1,0:T(8,128)(2,1)S(1)} %get-tuple-element.158, bf16[128,2048]{1,0:T(8,128)(2,1)S(1)} %get-tuple-element.157), kind=kOutput, calls=%fused_computation.66 | convolution fusion | flops 537919360 | bytes 6029824 | tf_op jit(solution)/shard_map/dot_general | solution.py:213
  63.3 4.8 %collective-permute-done.46 = bf16[1,64,2048]{2,1,0:T(8,128)(2,1)S(1)} collective-permute-done((bf16[1,64,2048]{2,1,0:T(8,128)(2,1)S(1)}, bf16[1,64,2048]{2,1,0:T(8,128)(2,1)S(1)}, u32[]{:S(2)}, u32[]{:S(2)}) %collective-permute-start.46) | collective-permute-done | bytes 262176 | tf_op jit(solution)/shard_map/ppermute | solution.py:294
  68.5 1.8 %collective-permute-start.48 = (bf16[2,64,2048]{2,1,0:T(8,128)(2,1)S(1)}, bf16[2,64,2048]{2,1,0:T(8,128)(2,1)}, u32[]{:S(2)}, u32[]{:S(2)}) collective-permute-start(bf16[2,64,2048]{2,1,0:T(8,128)(2,1)S(1)} %pad_maximum_fusion.4), channel_id=1, source_target_pairs={{0,2},{1,3},{2,0},{3,1},{4,6},{5,7},{6,4},{7,5},{8,10},{9,11},{10,... | collective-permute-start | bytes 1572872 | tf_op jit(solution)/shard_map/ppermute | solution.py:294
  70.4 1.7 %collective-permute-start.49 = (bf16[2,64,2048]{2,1,0:T(8,128)(2,1)S(1)}, bf16[2,64,2048]{2,1,0:T(8,128)(2,1)}, u32[]{:S(2)}, u32[]{:S(2)}) collective-permute-start(bf16[2,64,2048]{2,1,0:T(8,128)(2,1)S(1)} %pad_maximum_fusion.5), channel_id=1, source_target_pairs={{0,4},{1,5},{2,6},{3,7},{4,0},{5,1},{6,2},{7,3},{8,12},{9,13},{10,... | collective-permute-start | bytes 1572872 | tf_op jit(solution)/shard_map/ppermute | solution.py:294
  72.2 8.5 %collective-permute-done.48 = bf16[2,64,2048]{2,1,0:T(8,128)(2,1)} collective-permute-done((bf16[2,64,2048]{2,1,0:T(8,128)(2,1)S(1)}, bf16[2,64,2048]{2,1,0:T(8,128)(2,1)}, u32[]{:S(2)}, u32[]{:S(2)}) %collective-permute-start.48) | collective-permute-done | bytes 524320 | tf_op jit(solution)/shard_map/ppermute | solution.py:294
  83.5 1.5 %pad_maximum_fusion.1 = bf16[2,4,64,2048]{3,2,1,0:T(8,128)(2,1)} fusion(bf16[1,4,64,2048]{3,2,1,0:T(8,128)(2,1)S(1)} %bitcast.135, bf16[1,4,64,2048]{3,2,1,0:T(8,128)(2,1)S(1)} %bitcast.130), kind=kLoop, calls=%fused_computation.17 | loop fusion | flops 1048576 | bytes 4194304 | tf_op jit(solution)/shard_map/stack | solution.py:242
  86.9 2.7 %collective-permute-done.50 = bf16[2,4,64,2048]{3,2,1,0:T(8,128)(2,1)} collective-permute-done((bf16[2,4,64,2048]{3,2,1,0:T(8,128)(2,1)}, bf16[2,4,64,2048]{3,2,1,0:T(8,128)(2,1)}, u32[]{:S(2)}, u32[]{:S(2)}) %collective-permute-start.50) | collective-permute-done | bytes 2097184 | tf_op jit(solution)/shard_map/ppermute | solution.py:294
  89.6 3.5 %fusion.22 = f32[512,512]{1,0:T(8,128)S(1)} fusion(bf16[512,2048]{1,0:T(8,128)(2,1)} %bitcast.31, bf16[2,2048,512]{2,1,0:T(8,128)(2,1)} %param.81), kind=kOutput, calls=%fused_computation.34 | convolution fusion | flops 1073741824 | bytes 5242880 | tf_op jit(solution)/shard_map/dot_general | solution.py:222
  93.1 3.0 %fusion.12 = f32[512,512]{1,0:T(8,128)S(1)} fusion(bf16[512,2048]{1,0:T(8,128)(2,1)} %bitcast.31, bf16[2,2048,512]{2,1,0:T(8,128)(2,1)S(1)} %copy-done.7), kind=kOutput, calls=%fused_computation.24 | convolution fusion | flops 1073741824 | bytes 5242880 | tf_op jit(solution)/shard_map/dot_general | solution.py:222
  96.1 2.9 %multiply_convert_fusion.1 = bf16[512,512]{1,0:T(8,128)(2,1)S(1)} fusion(f32[512,512]{1,0:T(8,128)S(1)} %fusion.22, bf16[512,2048]{1,0:T(8,128)(2,1)} %bitcast.31, bf16[2,2048,512]{2,1,0:T(8,128)(2,1)S(1)} %copy-done.8), kind=kOutput, calls=%fused_computation.64 | convolution fusion | flops 1075314688 | bytes 5767168 | tf_op jit(solution)/shard_map/dot_general | solution.py:223
  99.0 3.1 %multiply_convert_fusion = bf16[512,512]{1,0:T(8,128)(2,1)S(1)} fusion(f32[512,512]{1,0:T(8,128)S(1)} %fusion.12, bf16[512,2048]{1,0:T(8,128)(2,1)} %bitcast.31, bf16[2,2048,512]{2,1,0:T(8,128)(2,1)S(1)} %copy-done.8), kind=kOutput, calls=%fused_computation.63 | convolution fusion | flops 1075314688 | bytes 5767168 | tf_op jit(solution)/shard_map/dot_general | solution.py:223
  103.4 1.4 add_convert_fusion
  106.3 1.4 fusion.44
  111.6 1.8 %convert_add_fusion = f32[512,2048]{1,0:T(8,128)S(1)} fusion(bf16[512,2048]{1,0:T(8,128)(2,1)S(1)} %collective-permute-done.51, bf16[512,2048]{1,0:T(8,128)(2,1)S(1)} %convolution_convert_fusion.2, bf16[512,512]{1,0:T(8,128)(2,1)S(1)} %fusion.47, f32[512]{0:T(512)S(1)} %bitcast.150, f32[512]{0:T(512)S(1)} %bitcast.149, bf16[2,512,2048]{2,1,0:T(8,128)(2,1)S(1)} %copy-done.9), kind=kOutput, calls=%fused_computation.9 | convolution fusion | flops 1082130432 | bytes 11014144 | tf_op jit(solution)/shard_map/dot_general | solution.py:226
  114.0 1.4 %collective-permute-start.52 = (bf16[2,64,2048]{2,1,0:T(8,128)(2,1)S(1)}, bf16[2,64,2048]{2,1,0:T(8,128)(2,1)S(1)}, u32[]{:S(2)}, u32[]{:S(2)}) collective-permute-start(bf16[2,64,2048]{2,1,0:T(8,128)(2,1)S(1)} %slice.274), channel_id=1, source_target_pairs={{0,2},{1,3},{2,0},{3,1},{4,6},{5,7},{6,4},{7,5},{8,10},{9,11},{10,... | collective-permute-start | bytes 1572872 | tf_op jit(solution)/shard_map/ppermute | solution.py:294
  115.5 1.5 %collective-permute-start.53 = (bf16[2,64,2048]{2,1,0:T(8,128)(2,1)S(1)}, bf16[2,64,2048]{2,1,0:T(8,128)(2,1)S(1)}, u32[]{:S(2)}, u32[]{:S(2)}) collective-permute-start(bf16[2,64,2048]{2,1,0:T(8,128)(2,1)S(1)} %slice.273), channel_id=1, source_target_pairs={{0,4},{1,5},{2,6},{3,7},{4,0},{5,1},{6,2},{7,3},{8,12},{9,13},{10,... | collective-permute-start | bytes 1572872 | tf_op jit(solution)/shard_map/ppermute | solution.py:294
  116.9 11.3 %collective-permute-done.52 = bf16[2,64,2048]{2,1,0:T(8,128)(2,1)S(1)} collective-permute-done((bf16[2,64,2048]{2,1,0:T(8,128)(2,1)S(1)}, bf16[2,64,2048]{2,1,0:T(8,128)(2,1)S(1)}, u32[]{:S(2)}, u32[]{:S(2)}) %collective-permute-start.52) | collective-permute-done | bytes 524320 | tf_op jit(solution)/shard_map/ppermute | solution.py:294
  129.6 1.5 %collective-permute-start.54 = (bf16[1,64,2048]{2,1,0:T(8,128)(2,1)S(1)}, bf16[1,64,2048]{2,1,0:T(8,128)(2,1)S(1)}, u32[]{:S(2)}, u32[]{:S(2)}) collective-permute-start(bf16[1,64,2048]{2,1,0:T(8,128)(2,1)S(1)} %slice.276), channel_id=1, source_target_pairs={{0,4},{1,5},{2,6},{3,7},{4,0},{5,1},{6,2},{7,3},{8,12},{9,13},{10,... | collective-permute-start | bytes 786440 | tf_op jit(solution)/shard_map/ppermute | solution.py:294
  131.8 5.3 %collective-permute-done.54 = bf16[1,64,2048]{2,1,0:T(8,128)(2,1)S(1)} collective-permute-done((bf16[1,64,2048]{2,1,0:T(8,128)(2,1)S(1)}, bf16[1,64,2048]{2,1,0:T(8,128)(2,1)S(1)}, u32[]{:S(2)}, u32[]{:S(2)}) %collective-permute-start.54) | collective-permute-done | bytes 262176 | tf_op jit(solution)/shard_map/ppermute | solution.py:294
  (101 shorter events, 25.4 us)
Async XLA Ops:
  0.0 8.1 %copy-start.3 = (s32[24,4]{0,1:T(4,128)S(1)}, s32[24,4]{0,1:T(4,128)}, u32[]{:S(2)}) copy-start(s32[24,4]{0,1:T(4,128)} %constant.74.clone) | copy-start | bytes 1156
  0.0 8.9 %copy-start = (bf16[128,2048]{1,0:T(8,128)(2,1)S(1)}, bf16[128,2048]{1,0:T(8,128)(2,1)}, u32[]{:S(2)}) copy-start(bf16[128,2048]{1,0:T(8,128)(2,1)} %param.69) | copy-start | bytes 1572868
  0.0 8.1 %copy-start.6 = (s32[4]{0:T(128)S(1)}, s32[4]{0:T(128)}, u32[]{:S(2)}) copy-start(s32[4]{0:T(128)} %param.76) | copy-start | bytes 52
  4.4 24.9 %all-to-all-start = ((bf16[8,774,128]{2,1,0:T(8,128)(2,1)}), bf16[8,774,128]{2,1,0:T(8,128)(2,1)S(1)}, u32[]{:S(2)}, u32[]{:S(2)}) async-start(bf16[8,774,128]{2,1,0:T(8,128)(2,1)} %shard_map.253), calls=%async_computation | async-start | bytes 3178496 | tf_op jit(solution)/shard_map/all_to_all | solution.py:100
  9.5 17.0 %copy-start.10 = (s32[4]{0:T(128)S(1)}, s32[4]{0:T(128)}, u32[]{:S(2)}) copy-start(s32[4]{0:T(128)} %param.75) | copy-start | bytes 52
  9.6 16.2 %collective-permute-start.1 = (bf16[128,2048]{1,0:T(8,128)(2,1)S(1)}, bf16[128,2048]{1,0:T(8,128)(2,1)S(1)}, u32[]{:S(2)}, u32[]{:S(2)}) collective-permute-start(bf16[128,2048]{1,0:T(8,128)(2,1)S(1)} %param.2), channel_id=1, source_target_pairs={{0,0},{8,16},{16,8},{24,24},{1,1},{9,17},{17,9},{25,25},{2,2},{10,... | collective-permute-start | bytes 1572872 | tf_op jit(solution)/shard_map/cond/branch_2_fun/ppermute | solution.py:344
  37.8 10.3 %all-to-all-start.1 = ((bf16[8,128,128]{1,2,0:T(8,128)(2,1)}), bf16[8,128,128]{1,2,0:T(8,128)(2,1)S(1)}, u32[]{:S(2)}, u32[]{:S(2)}) async-start(bf16[8,128,128]{1,2,0:T(8,128)(2,1)} %copy.75), calls=%async_computation.1 | async-start | bytes 524288 | tf_op jit(solution)/shard_map/all_to_all | solution.py:132
  48.3 9.6 %collective-permute-start.24 = (bf16[134,1024]{1,0:T(8,128)(2,1)S(1)}, bf16[134,1024]{1,0:T(8,128)(2,1)S(1)}, u32[]{:S(2)}, u32[]{:S(2)}) collective-permute-start(bf16[134,1024]{1,0:T(8,128)(2,1)S(1)} %param.26), channel_id=1, source_target_pairs={{0,0},{8,16},{16,8},{24,24},{1,1},{9,17},{17,9},{25,25},{2,2},{10,... | collective-permute-start | bytes 823304 | tf_op jit(solution)/shard_map/cond/branch_2_fun/ppermute | solution.py:344
  58.2 3.1 %copy-start.2 = (f32[2048]{0:T(1024)S(1)}, f32[2048]{0:T(1024)}, u32[]{:S(2)}) copy-start(f32[2048]{0:T(1024)} %param.78) | copy-start | bytes 24580
  58.2 12.1 %copy-start.4 = (s32[8]{0:T(128)S(1)}, s32[8]{0:T(128)}, u32[]{:S(2)}) copy-start(s32[8]{0:T(128)} %constant.76.clone) | copy-start | bytes 100
  58.2 12.1 %copy-start.5 = (s32[8]{0:T(128)S(1)}, s32[8]{0:T(128)}, u32[]{:S(2)}) copy-start(s32[8]{0:T(128)} %constant.75.clone) | copy-start | bytes 100
  61.5 6.5 %collective-permute-start.46 = (bf16[1,64,2048]{2,1,0:T(8,128)(2,1)S(1)}, bf16[1,64,2048]{2,1,0:T(8,128)(2,1)S(1)}, u32[]{:S(2)}, u32[]{:S(2)}) collective-permute-start(bf16[1,64,2048]{2,1,0:T(8,128)(2,1)S(1)} %get-tuple-element.137), channel_id=1, source_target_pairs={{0,4},{1,5},{2,6},{3,7},{4,0},{5,1},{6,2},{7,3},{8,12},{9,13},{10,... | collective-permute-start | bytes 786440 | tf_op jit(solution)/shard_map/ppermute | solution.py:294
  62.1 6.4 %collective-permute-start.47 = (bf16[1,64,2048]{2,1,0:T(8,128)(2,1)S(1)}, bf16[1,64,2048]{2,1,0:T(8,128)(2,1)S(1)}, u32[]{:S(2)}, u32[]{:S(2)}) collective-permute-start(bf16[1,64,2048]{2,1,0:T(8,128)(2,1)S(1)} %get-tuple-element.136), channel_id=1, source_target_pairs={{0,2},{1,3},{2,0},{3,1},{4,6},{5,7},{6,4},{7,5},{8,10},{9,11},{10,... | collective-permute-start | bytes 786440 | tf_op jit(solution)/shard_map/ppermute | solution.py:294
  68.5 13.3 %copy-start.1 = (bf16[2,64,2048]{2,1,0:T(8,128)(2,1)}, bf16[2,64,2048]{2,1,0:T(8,128)(2,1)S(1)}, u32[]{:S(2)}) copy-start(bf16[2,64,2048]{2,1,0:T(8,128)(2,1)S(1)} %pad_maximum_fusion.5) | copy-start | bytes 1572868
  68.5 12.1 %collective-permute-start.48 = (bf16[2,64,2048]{2,1,0:T(8,128)(2,1)S(1)}, bf16[2,64,2048]{2,1,0:T(8,128)(2,1)}, u32[]{:S(2)}, u32[]{:S(2)}) collective-permute-start(bf16[2,64,2048]{2,1,0:T(8,128)(2,1)S(1)} %pad_maximum_fusion.4), channel_id=1, source_target_pairs={{0,2},{1,3},{2,0},{3,1},{4,6},{5,7},{6,4},{7,5},{8,10},{9,11},{10,... | collective-permute-start | bytes 1572872 | tf_op jit(solution)/shard_map/ppermute | solution.py:294
  70.4 11.9 %collective-permute-start.49 = (bf16[2,64,2048]{2,1,0:T(8,128)(2,1)S(1)}, bf16[2,64,2048]{2,1,0:T(8,128)(2,1)}, u32[]{:S(2)}, u32[]{:S(2)}) collective-permute-start(bf16[2,64,2048]{2,1,0:T(8,128)(2,1)S(1)} %pad_maximum_fusion.5), channel_id=1, source_target_pairs={{0,4},{1,5},{2,6},{3,7},{4,0},{5,1},{6,2},{7,3},{8,12},{9,13},{10,... | collective-permute-start | bytes 1572872 | tf_op jit(solution)/shard_map/ppermute | solution.py:294
  85.1 4.5 %collective-permute-start.50 = (bf16[2,4,64,2048]{3,2,1,0:T(8,128)(2,1)}, bf16[2,4,64,2048]{3,2,1,0:T(8,128)(2,1)}, u32[]{:S(2)}, u32[]{:S(2)}) collective-permute-start(bf16[2,4,64,2048]{3,2,1,0:T(8,128)(2,1)} %pad_maximum_fusion.1), channel_id=1, source_target_pairs={{0,1},{1,0},{2,3},{3,2},{4,5},{5,4},{6,7},{7,6},{8,9},{9,8},{10,11... | collective-permute-start | bytes 6291464 | tf_op jit(solution)/shard_map/ppermute | solution.py:294
  86.8 6.2 %copy-start.7 = (bf16[2,2048,512]{2,1,0:T(8,128)(2,1)S(1)}, bf16[2,2048,512]{2,1,0:T(8,128)(2,1)}, u32[]{:S(2)}) copy-start(bf16[2,2048,512]{2,1,0:T(8,128)(2,1)} %param.81) | copy-start | bytes 12582916
  93.1 3.0 %copy-start.8 = (bf16[2,2048,512]{2,1,0:T(8,128)(2,1)S(1)}, bf16[2,2048,512]{2,1,0:T(8,128)(2,1)}, u32[]{:S(2)}) copy-start(bf16[2,2048,512]{2,1,0:T(8,128)(2,1)} %param.82) | copy-start | bytes 12582916
  99.0 3.1 %copy-start.9 = (bf16[2,512,2048]{2,1,0:T(8,128)(2,1)S(1)}, bf16[2,512,2048]{2,1,0:T(8,128)(2,1)}, u32[]{:S(2)}) copy-start(bf16[2,512,2048]{2,1,0:T(8,128)(2,1)} %param.83) | copy-start | bytes 12582916
  104.8 6.7 %collective-permute-start.51 = (bf16[512,2048]{1,0:T(8,128)(2,1)S(1)}, bf16[512,2048]{1,0:T(8,128)(2,1)S(1)}, u32[]{:S(2)}, u32[]{:S(2)}) collective-permute-start(bf16[512,2048]{1,0:T(8,128)(2,1)S(1)} %add_convert_fusion), channel_id=1, source_target_pairs={{0,1},{1,0},{2,3},{3,2},{4,5},{5,4},{6,7},{7,6},{8,9},{9,8},{10,11... | collective-permute-start | bytes 6291464 | tf_op jit(solution)/shard_map/ppermute | solution.py:294
  114.0 14.3 %collective-permute-start.52 = (bf16[2,64,2048]{2,1,0:T(8,128)(2,1)S(1)}, bf16[2,64,2048]{2,1,0:T(8,128)(2,1)S(1)}, u32[]{:S(2)}, u32[]{:S(2)}) collective-permute-start(bf16[2,64,2048]{2,1,0:T(8,128)(2,1)S(1)} %slice.274), channel_id=1, source_target_pairs={{0,2},{1,3},{2,0},{3,1},{4,6},{5,7},{6,4},{7,5},{8,10},{9,11},{10,... | collective-permute-start | bytes 1572872 | tf_op jit(solution)/shard_map/ppermute | solution.py:294
  115.5 14.0 %collective-permute-start.53 = (bf16[2,64,2048]{2,1,0:T(8,128)(2,1)S(1)}, bf16[2,64,2048]{2,1,0:T(8,128)(2,1)S(1)}, u32[]{:S(2)}, u32[]{:S(2)}) collective-permute-start(bf16[2,64,2048]{2,1,0:T(8,128)(2,1)S(1)} %slice.273), channel_id=1, source_target_pairs={{0,4},{1,5},{2,6},{3,7},{4,0},{5,1},{6,2},{7,3},{8,12},{9,13},{10,... | collective-permute-start | bytes 1572872 | tf_op jit(solution)/shard_map/ppermute | solution.py:294
  129.6 7.5 %collective-permute-start.54 = (bf16[1,64,2048]{2,1,0:T(8,128)(2,1)S(1)}, bf16[1,64,2048]{2,1,0:T(8,128)(2,1)S(1)}, u32[]{:S(2)}, u32[]{:S(2)}) collective-permute-start(bf16[1,64,2048]{2,1,0:T(8,128)(2,1)S(1)} %slice.276), channel_id=1, source_target_pairs={{0,4},{1,5},{2,6},{3,7},{4,0},{5,1},{6,2},{7,3},{8,12},{9,13},{10,... | collective-permute-start | bytes 786440 | tf_op jit(solution)/shard_map/ppermute | solution.py:294
  131.1 7.2 %collective-permute-start.55 = (bf16[1,64,2048]{2,1,0:T(8,128)(2,1)S(1)}, bf16[1,64,2048]{2,1,0:T(8,128)(2,1)S(1)}, u32[]{:S(2)}, u32[]{:S(2)}) collective-permute-start(bf16[1,64,2048]{2,1,0:T(8,128)(2,1)S(1)} %slice.275), channel_id=1, source_target_pairs={{0,2},{1,3},{2,0},{3,1},{4,6},{5,7},{6,4},{7,5},{8,10},{9,11},{10,... | collective-permute-start | bytes 786440 | tf_op jit(solution)/shard_map/ppermute | solution.py:294

commit v3 on v2

--- a/solution.py
+++ b/solution.py
@@ -239,7 +239,8 @@
         inputs = [normed[f : f + stream_rows] for f in firsts]
         helds = gather_xor(inputs, [order[:-1] for order in orders], ctx_count)
         last_mask = 1 << orders[0][-1]
-        arrived = swap(jnp.stack(helds), last_mask, ctx_count)
+        held = jnp.stack(helds)
+        arrived = swap(held, last_mask, ctx_count)
         half_blocks = ctx_count // 2
         gates_own, gates_arrived = [], []
         for first, order in zip(firsts, orders):
@@ -247,17 +248,11 @@
             gates = jnp.take(local_gates[:, :, first : first + stream_rows], sources, axis=1)
             gates_own.append(gates[:, :half_blocks].reshape(local_experts, -1))
             gates_arrived.append(gates[:, half_blocks:].reshape(local_experts, -1))
-        half_rows = half_blocks * stream_rows
-        own_part = experts_on(
-            jnp.concatenate([held.reshape(half_rows, feature_width) for held in helds], 0),
-            jnp.concatenate(gates_own, 1),
-        )
-        arrived_part = experts_on(
-            arrived.reshape(2 * half_rows, feature_width), jnp.concatenate(gates_arrived, 1)
-        )
-        returned = swap(arrived_part.astype(jnp.bfloat16), last_mask, ctx_count)
-        totals = own_part + returned.astype(jnp.float32)
-        totals = totals.reshape(2, half_blocks, stream_rows, feature_width)
+        rows = jnp.concatenate([held, arrived], 0).reshape(-1, feature_width)
+        part = experts_on(rows, jnp.concatenate(gates_own + gates_arrived, 1))
+        part = part.reshape(2, 2, half_blocks, stream_rows, feature_width)
+        returned = swap(part[1].astype(jnp.bfloat16), last_mask, ctx_count)
+        totals = part[0] + returned.astype(jnp.float32)
         totals = list(lax.optimization_barrier((totals[0], totals[1])))
         moe_pieces = reduce_xor(totals, orders, ctx_count, steps - 1)
         moe_rows = jnp.concatenate(moe_pieces, 0)

time: 141 us -> 138 us (0.979)
  the two profiles are of different devices: /device:TPU:16 before, /device:TPU:0 now
where the time goes in v3:
time: 138 us; the launch traced here: 140 us
  waiting for transfers between devices  70.7 us (51%)
  starting transfers between devices  23.2 us (17%)
  matrix products  22.5 us (16%)
  other arithmetic  14.7 us (11%)
  local copies, waits for them, and re-layouts  4.76 us (3%)
  Pallas kernels  2.96 us (2%)
    ppermute x10, waiting for transfers between devices, swap(): return lax.ppermute(rows, 'ctx', [(c, c ^ mask) for c in range(ctx_count)])  42.3 us
    ppermute x2, waiting for transfers between devices, mover(): return lambda rows: lax.ppermute(rows, 'req', pairs)  21.5 us
    ppermute x2, starting transfers between devices, mover(): return lambda rows: lax.ppermute(rows, 'req', pairs)  8.02 us
    all_to_all x1, waiting for transfers between devices, attend_by_head(): lax.all_to_all(head_out, 'ctx', split_axis=0, concat_axis=0, tiled=True)  6.89 us
    ppermute x10, starting transfers between devices, swap(): return lax.ppermute(rows, 'ctx', [(c, c ^ mask) for c in range(ctx_count)])  6.18 us
    all_to_all x1, starting transfers between devices, attend_by_head(): got = lax.all_to_all(packed, 'ctx', split_axis=0, concat_axis=0, tiled=True)  5.17 us
    dot_general x2, matrix products, experts_on(): up_val = jnp.dot(rows, up_proj[j], preferred_element_type=jnp.float32)  5.16 us
    dot_general x2, matrix products, experts_on(): jnp.dot(activated, down_proj[j], preferred_element_type=jnp.float32)  4.83 us
  transfers between devices with their start and end apart: 14, of which 11 were waited for; matrix products, arithmetic and copies ran while one was open for 5% of the time, Pallas kernels for 0%

profile of v3, /device:TPU:0, one launch (start us, length us, event | category | flops | bytes accessed | tf_op | source)
XLA Modules:
  0.0 140.2 jit_solution(17460818573145443258)
XLA Ops:
  1.4 3.0 %shard_map.253 = bf16[8,774,128]{2,1,0:T(8,128)(2,1)} custom-call(bf16[128,1024]{1,0:T(8,128)(2,1)} %refs_0_.1, bf16[128,1024]{1,0:T(8,128)(2,1)} %refs_1_.1, bf16[192,1024]{1,0:T(8,128)(2,1)} %refs_2_.1, bf16[128,1024]{1,0:T(8,128)(2,1)} %refs_3_.1, bf16[192,1024]{1,0:T(8,128)(2,1)} %refs_4_.1, bf16[8,6,128]{2,1,0:T(8,128)(2,1)} %copy.74.refs_5_), custom_call_target="tpu_custom_call" | custom-call | bytes 3170304 | tf_op jit(solution)/shard_map/pallas_call | solution.py:76
  4.4 5.2 %all-to-all-start = ((bf16[8,774,128]{2,1,0:T(8,128)(2,1)}), bf16[8,774,128]{2,1,0:T(8,128)(2,1)S(1)}, u32[]{:S(2)}, u32[]{:S(2)}) async-start(bf16[8,774,128]{2,1,0:T(8,128)(2,1)} %shard_map.253), calls=%async_computation | async-start | bytes 3178496 | tf_op jit(solution)/shard_map/all_to_all | solution.py:100
  11.0 18.2 %conditional.2 = (bf16[128,2048]{1,0:T(8,128)(2,1)S(1)}) conditional(s32[]{:T(128)} %clamp.6, bf16[128,2048]{1,0:T(8,128)(2,1)S(1)} %copy-done, bf16[128,2048]{1,0:T(8,128)(2,1)S(1)} %copy-done, bf16[128,2048]{1,0:T(8,128)(2,1)S(1)} %copy-done, bf16[128,2048]{1,0:T(8,128)(2,1)S(1)} %copy-done, ...), branch_computations={%region_3.4_spmd, %region_4.5_spmd, %region_5.6_spmd, %region_6.7_... | conditional | bytes 3145776 | solution.py:341
  11.0 4.5 %collective-permute-start.14 = (bf16[128,2048]{1,0:T(8,128)(2,1)S(1)}, bf16[128,2048]{1,0:T(8,128)(2,1)S(1)}, u32[]{:S(2)}, u32[]{:S(2)}) collective-permute-start(bf16[128,2048]{1,0:T(8,128)(2,1)S(1)} %param.15), channel_id=1, source_target_pairs={{0,16},{8,8},{16,24},{24,0},{1,17},{9,9},{17,25},{25,1},{2,18},{10... | collective-permute-start | bytes 1572872 | tf_op jit(solution)/shard_map/cond/branch_15_fun/ppermute | solution.py:339
  15.5 13.6 %collective-permute-done.14 = bf16[128,2048]{1,0:T(8,128)(2,1)S(1)} collective-permute-done((bf16[128,2048]{1,0:T(8,128)(2,1)S(1)}, bf16[128,2048]{1,0:T(8,128)(2,1)S(1)}, u32[]{:S(2)}, u32[]{:S(2)}) %collective-permute-start.14) | collective-permute-done | bytes 524320 | tf_op jit(solution)/shard_map/cond/branch_15_fun/ppermute | solution.py:339
  29.8 1.4 fusion.53
  32.0 1.8 %fusion = (f32[1024]{0:T(1024)S(1)}, f32[1024,2560]{1,0:T(8,128)S(1)}) fusion(pred[2560]{0:T(1024)(128)(4,1)S(1)} %fusion.47, bf16[1024,128]{1,0:T(8,128)(2,1)S(1)} %bitcast.117, bf16[2560,128]{1,0:T(8,128)(2,1)S(1)} %bitcast.113), kind=kOutput, calls=%fused_computation.4 | convolution fusion | flops 678951936 | bytes 11409920 | tf_op jit(solution)/shard_map/thd,phd->htp/dot_general | solution.py:117
  33.9 2.7 %fusion.1 = f32[1024]{0:T(1024)S(1)} fusion(f32[1024,2560]{1,0:T(8,128)S(1)} %get-tuple-element.150, f32[1024]{0:T(1024)S(1)} %get-tuple-element.149, pred[2560]{0:T(1024)(128)(4,1)S(1)} %fusion.47), kind=kLoop, calls=%fused_computation.6 | loop fusion | flops 13106176 | bytes 10496512 | tf_op jit(solution)/shard_map/reduce_sum | solution.py:123
  36.5 3.0 %fusion.33 = bf16[16,8,8,128]{3,1,2,0:T(8,128)(2,1)S(1)} fusion(bf16[2560,128]{1,0:T(8,128)(2,1)S(1)} %bitcast.120, f32[1024,2560]{1,0:T(8,128)S(1)} %get-tuple-element.150, f32[1024]{0:T(1024)S(1)} %get-tuple-element.149, pred[2560]{0:T(1024)(128)(4,1)S(1)} %fusion.47, f32[1024]{0:T(1024)S(1)} %fusion.1), kind=kOutput, calls=%fused_computation.49 | convolution fusion | flops 684457984 | bytes 11414016 | tf_op jit(solution)/shard_map/htp,phd->thd/dot_general | solution.py:124
  40.3 3.8 %all-to-all-start.1 = ((bf16[8,128,128]{1,2,0:T(8,128)(2,1)}), bf16[8,128,128]{1,2,0:T(8,128)(2,1)S(1)}, u32[]{:S(2)}, u32[]{:S(2)}) async-start(bf16[8,128,128]{1,2,0:T(8,128)(2,1)} %copy.75), calls=%async_computation.1 | async-start | bytes 524288 | tf_op jit(solution)/shard_map/all_to_all | solution.py:132
  44.2 6.9 %all-to-all-done.1 = bf16[8,128,128]{1,2,0:T(8,128)(2,1)S(1)} async-done(((bf16[8,128,128]{1,2,0:T(8,128)(2,1)}), bf16[8,128,128]{1,2,0:T(8,128)(2,1)S(1)}, u32[]{:S(2)}, u32[]{:S(2)}) %all-to-all-start.1) | async-done | bytes 262176 | tf_op jit(solution)/shard_map/all_to_all | solution.py:132
  51.3 11.7 %conditional.3 = (bf16[134,1024]{1,0:T(8,128)(2,1)S(1)}) conditional(s32[]{:T(128)} %clamp.6, bf16[134,1024]{1,0:T(8,128)(2,1)S(1)} %pad_maximum_fusion.6, bf16[134,1024]{1,0:T(8,128)(2,1)S(1)} %pad_maximum_fusion.6, bf16[134,1024]{1,0:T(8,128)(2,1)S(1)} %pad_maximum_fusion.6, ...), branch_computations={%region_33.34_spmd, %region_34.35_spmd, %region_35.36_spmd, %regio... | conditional | bytes 1646640 | solution.py:341
  51.5 3.5 %collective-permute-start.37 = (bf16[134,1024]{1,0:T(8,128)(2,1)S(1)}, bf16[134,1024]{1,0:T(8,128)(2,1)S(1)}, u32[]{:S(2)}, u32[]{:S(2)}) collective-permute-start(bf16[134,1024]{1,0:T(8,128)(2,1)S(1)} %param.39), channel_id=1, source_target_pairs={{0,16},{8,8},{16,24},{24,0},{1,17},{9,9},{17,25},{25,1},{2,18},{10... | collective-permute-start | bytes 823304 | tf_op jit(solution)/shard_map/cond/branch_15_fun/ppermute | solution.py:339
  55.1 7.9 %collective-permute-done.37 = bf16[134,1024]{1,0:T(8,128)(2,1)S(1)} collective-permute-done((bf16[134,1024]{1,0:T(8,128)(2,1)S(1)}, bf16[134,1024]{1,0:T(8,128)(2,1)S(1)}, u32[]{:S(2)}, u32[]{:S(2)}) %collective-permute-start.37) | collective-permute-done | bytes 274464 | tf_op jit(solution)/shard_map/cond/branch_15_fun/ppermute | solution.py:339
  63.1 3.0 %multiply_reduce_fusion = (f32[128]{0:T(128)S(1)}, f32[128,2048]{1,0:T(8,128)S(1)}) fusion(bf16[1024,2048]{1,0:T(8,128)(2,1)} %param.77, bf16[134,1024]{1,0:T(8,128)(2,1)S(1)} %get-tuple-element.156, bf16[128,2048]{1,0:T(8,128)(2,1)S(1)} %get-tuple-element.155), kind=kOutput, calls=%fused_computation.46 | convolution fusion | flops 537919360 | bytes 6029824 | tf_op jit(solution)/shard_map/dot_general | solution.py:213
  66.3 1.4 collective-permute-start.47
  68.1 5.1 %collective-permute-done.47 = bf16[1,64,2048]{2,1,0:T(8,128)(2,1)S(1)} collective-permute-done((bf16[1,64,2048]{2,1,0:T(8,128)(2,1)S(1)}, bf16[1,64,2048]{2,1,0:T(8,128)(2,1)S(1)}, u32[]{:S(2)}, u32[]{:S(2)}) %collective-permute-start.47) | collective-permute-done | bytes 262176 | tf_op jit(solution)/shard_map/ppermute | solution.py:289
  73.3 1.4 collective-permute-done.46
  75.5 11.1 %collective-permute-done.48 = bf16[2,64,2048]{2,1,0:T(8,128)(2,1)} collective-permute-done((bf16[2,64,2048]{2,1,0:T(8,128)(2,1)S(1)}, bf16[2,64,2048]{2,1,0:T(8,128)(2,1)}, u32[]{:S(2)}, u32[]{:S(2)}) %collective-permute-start.48) | collective-permute-done | bytes 524320 | tf_op jit(solution)/shard_map/ppermute | solution.py:289
  88.9 1.5 %pad_maximum_fusion.1 = bf16[2,4,64,2048]{3,2,1,0:T(8,128)(2,1)} fusion(bf16[1,4,64,2048]{3,2,1,0:T(8,128)(2,1)S(1)} %bitcast.104, bf16[1,4,64,2048]{3,2,1,0:T(8,128)(2,1)S(1)} %bitcast.102), kind=kLoop, calls=%fused_computation.16 | loop fusion | flops 1048576 | bytes 4194304 | tf_op jit(solution)/shard_map/stack | solution.py:242
  92.3 2.6 %collective-permute-done.50 = bf16[2,4,64,2048]{3,2,1,0:T(8,128)(2,1)} collective-permute-done((bf16[2,4,64,2048]{3,2,1,0:T(8,128)(2,1)}, bf16[2,4,64,2048]{3,2,1,0:T(8,128)(2,1)}, u32[]{:S(2)}, u32[]{:S(2)}) %collective-permute-start.50) | collective-permute-done | bytes 2097184 | tf_op jit(solution)/shard_map/ppermute | solution.py:289
  94.9 1.8 %pad_maximum_fusion = bf16[4,4,64,2048]{3,2,1,0:T(8,128)(2,1)S(1)} fusion(bf16[2,4,64,2048]{3,2,1,0:T(8,128)(2,1)} %collective-permute-done.50, bf16[1,4,64,2048]{3,2,1,0:T(8,128)(2,1)S(1)} %bitcast.105, bf16[1,4,64,2048]{3,2,1,0:T(8,128)(2,1)S(1)} %bitcast.103), kind=kLoop, calls=%fused_computation.11 | loop fusion | flops 4194304 | bytes 8388608 | tf_op jit(solution)/shard_map/concatenate | solution.py:251
  96.7 2.3 %fusion.9 = f32[1024,512]{1,0:T(8,128)S(1)} fusion(bf16[1024,2048]{1,0:T(8,128)(2,1)S(1)} %bitcast.109, bf16[2,2048,512]{2,1,0:T(8,128)(2,1)S(1)} %copy-done.7), kind=kOutput, calls=%fused_computation.20 | convolution fusion | flops 2147483648 | bytes 8388608 | tf_op jit(solution)/shard_map/dot_general | solution.py:222
  99.0 2.3 %fusion.15 = f32[1024,512]{1,0:T(8,128)S(1)} fusion(bf16[1024,2048]{1,0:T(8,128)(2,1)S(1)} %bitcast.110, bf16[2,2048,512]{2,1,0:T(8,128)(2,1)S(1)} %copy-done.7), kind=kOutput, calls=%fused_computation.26 | convolution fusion | flops 2147483648 | bytes 8388608 | tf_op jit(solution)/shard_map/dot_general | solution.py:222
  101.4 2.6 %multiply_convert_fusion = bf16[1024,512]{1,0:T(8,128)(2,1)S(1)} fusion(f32[1024,512]{1,0:T(8,128)S(1)} %fusion.9, bf16[1024,2048]{1,0:T(8,128)(2,1)S(1)} %bitcast.111, bf16[2,2048,512]{2,1,0:T(8,128)(2,1)S(1)} %copy-done.8), kind=kOutput, calls=%fused_computation.29 | convolution fusion | flops 2150629376 | bytes 9437184 | tf_op jit(solution)/shard_map/dot_general | solution.py:223
  104.0 2.6 %multiply_convert_fusion.1 = bf16[1024,512]{1,0:T(8,128)(2,1)S(1)} fusion(f32[1024,512]{1,0:T(8,128)S(1)} %fusion.15, bf16[1024,2048]{1,0:T(8,128)(2,1)S(1)} %bitcast.112, bf16[2,2048,512]{2,1,0:T(8,128)(2,1)S(1)} %copy-done.8), kind=kOutput, calls=%fused_computation.33 | convolution fusion | flops 2150629376 | bytes 9437184 | tf_op jit(solution)/shard_map/dot_general | solution.py:223
  106.6 2.3 %fusion.11 = bf16[1024,2048]{1,0:T(8,128)(2,1)S(1)} fusion(bf16[1024,512]{1,0:T(8,128)(2,1)S(1)} %multiply_convert_fusion.1, bf16[2,512,2048]{2,1,0:T(8,128)(2,1)S(1)} %copy-done.9), kind=kOutput, calls=%fused_computation.22 | convolution fusion | flops 2147483648 | bytes 7340032 | tf_op jit(solution)/shard_map/dot_general | solution.py:226
  108.9 2.5 %multiply_add_fusion = f32[1024,2048]{1,0:T(8,128)S(1)} fusion(f32[1024]{0:T(1024)S(1)} %bitcast.124, bf16[1024,2048]{1,0:T(8,128)(2,1)S(1)} %fusion.11, f32[1024]{0:T(1024)S(1)} %bitcast.123, bf16[1024,512]{1,0:T(8,128)(2,1)S(1)} %multiply_convert_fusion, bf16[2,512,2048]{2,1,0:T(8,128)(2,1)S(1)} %copy-done.9), kind=kOutput, calls=%fused_computation.5 | convolution fusion | flops 2160066560 | bytes 15736832 | tf_op jit(solution)/shard_map/dot_general | solution.py:226
  112.4 3.5 %collective-permute-done.51 = bf16[2,4,64,2048]{3,2,1,0:T(8,128)(2,1)S(1)} collective-permute-done((bf16[2,4,64,2048]{3,2,1,0:T(8,128)(2,1)S(1)}, bf16[2,4,64,2048]{3,2,1,0:T(8,128)(2,1)S(1)}, u32[]{:S(2)}, u32[]{:S(2)}) %collective-permute-start.51) | collective-permute-done | bytes 2097184 | tf_op jit(solution)/shard_map/ppermute | solution.py:289
  117.9 13.1 %collective-permute-done.53 = bf16[2,64,2048]{2,1,0:T(8,128)(2,1)S(1)} collective-permute-done((bf16[2,64,2048]{2,1,0:T(8,128)(2,1)S(1)}, bf16[2,64,2048]{2,1,0:T(8,128)(2,1)S(1)}, u32[]{:S(2)}, u32[]{:S(2)}) %collective-permute-start.53) | collective-permute-done | bytes 524320 | tf_op jit(solution)/shard_map/ppermute | solution.py:289
  132.0 1.8 %collective-permute-start.54 = (bf16[1,64,2048]{2,1,0:T(8,128)(2,1)S(1)}, bf16[1,64,2048]{2,1,0:T(8,128)(2,1)S(1)}, u32[]{:S(2)}, u32[]{:S(2)}) collective-permute-start(bf16[1,64,2048]{2,1,0:T(8,128)(2,1)S(1)} %slice.243), channel_id=1, source_target_pairs={{0,4},{1,5},{2,6},{3,7},{4,0},{5,1},{6,2},{7,3},{8,12},{9,13},{10,... | collective-permute-start | bytes 786440 | tf_op jit(solution)/shard_map/ppermute | solution.py:289
  133.8 5.0 %collective-permute-done.55 = bf16[1,64,2048]{2,1,0:T(8,128)(2,1)S(1)} collective-permute-done((bf16[1,64,2048]{2,1,0:T(8,128)(2,1)S(1)}, bf16[1,64,2048]{2,1,0:T(8,128)(2,1)S(1)}, u32[]{:S(2)}, u32[]{:S(2)}) %collective-permute-start.55) | collective-permute-done | bytes 262176 | tf_op jit(solution)/shard_map/ppermute | solution.py:289
  (98 shorter events, 15.6 us)
Async XLA Ops:
  0.0 9.6 %copy-start.3 = (s32[24,4]{0,1:T(4,128)S(1)}, s32[24,4]{0,1:T(4,128)}, u32[]{:S(2)}) copy-start(s32[24,4]{0,1:T(4,128)} %constant.72.clone) | copy-start | bytes 1156
  0.0 10.3 %copy-start = (bf16[128,2048]{1,0:T(8,128)(2,1)S(1)}, bf16[128,2048]{1,0:T(8,128)(2,1)}, u32[]{:S(2)}) copy-start(bf16[128,2048]{1,0:T(8,128)(2,1)} %param.69) | copy-start | bytes 1572868
  0.0 9.6 %copy-start.6 = (s32[4]{0:T(128)S(1)}, s32[4]{0:T(128)}, u32[]{:S(2)}) copy-start(s32[4]{0:T(128)} %param.76) | copy-start | bytes 52
  4.4 27.5 %all-to-all-start = ((bf16[8,774,128]{2,1,0:T(8,128)(2,1)}), bf16[8,774,128]{2,1,0:T(8,128)(2,1)S(1)}, u32[]{:S(2)}, u32[]{:S(2)}) async-start(bf16[8,774,128]{2,1,0:T(8,128)(2,1)} %shard_map.253), calls=%async_computation | async-start | bytes 3178496 | tf_op jit(solution)/shard_map/all_to_all | solution.py:100
  11.0 18.8 %copy-start.10 = (s32[4]{0:T(128)S(1)}, s32[4]{0:T(128)}, u32[]{:S(2)}) copy-start(s32[4]{0:T(128)} %param.75) | copy-start | bytes 52
  11.0 18.1 %collective-permute-start.14 = (bf16[128,2048]{1,0:T(8,128)(2,1)S(1)}, bf16[128,2048]{1,0:T(8,128)(2,1)S(1)}, u32[]{:S(2)}, u32[]{:S(2)}) collective-permute-start(bf16[128,2048]{1,0:T(8,128)(2,1)S(1)} %param.15), channel_id=1, source_target_pairs={{0,16},{8,8},{16,24},{24,0},{1,17},{9,9},{17,25},{25,1},{2,18},{10... | collective-permute-start | bytes 1572872 | tf_op jit(solution)/shard_map/cond/branch_15_fun/ppermute | solution.py:339
  40.3 10.8 %all-to-all-start.1 = ((bf16[8,128,128]{1,2,0:T(8,128)(2,1)}), bf16[8,128,128]{1,2,0:T(8,128)(2,1)S(1)}, u32[]{:S(2)}, u32[]{:S(2)}) async-start(bf16[8,128,128]{1,2,0:T(8,128)(2,1)} %copy.75), calls=%async_computation.1 | async-start | bytes 524288 | tf_op jit(solution)/shard_map/all_to_all | solution.py:132
  51.5 11.4 %collective-permute-start.37 = (bf16[134,1024]{1,0:T(8,128)(2,1)S(1)}, bf16[134,1024]{1,0:T(8,128)(2,1)S(1)}, u32[]{:S(2)}, u32[]{:S(2)}) collective-permute-start(bf16[134,1024]{1,0:T(8,128)(2,1)S(1)} %param.39), channel_id=1, source_target_pairs={{0,16},{8,8},{16,24},{24,0},{1,17},{9,9},{17,25},{25,1},{2,18},{10... | collective-permute-start | bytes 823304 | tf_op jit(solution)/shard_map/cond/branch_15_fun/ppermute | solution.py:339
  63.0 3.1 %copy-start.2 = (f32[2048]{0:T(1024)S(1)}, f32[2048]{0:T(1024)}, u32[]{:S(2)}) copy-start(f32[2048]{0:T(1024)} %param.78) | copy-start | bytes 24580
  63.0 12.4 %copy-start.4 = (s32[8]{0:T(128)S(1)}, s32[8]{0:T(128)}, u32[]{:S(2)}) copy-start(s32[8]{0:T(128)} %constant.74.clone) | copy-start | bytes 100
  63.0 12.4 %copy-start.5 = (s32[8]{0:T(128)S(1)}, s32[8]{0:T(128)}, u32[]{:S(2)}) copy-start(s32[8]{0:T(128)} %constant.73.clone) | copy-start | bytes 100
  66.3 6.9 %collective-permute-start.47 = (bf16[1,64,2048]{2,1,0:T(8,128)(2,1)S(1)}, bf16[1,64,2048]{2,1,0:T(8,128)(2,1)S(1)}, u32[]{:S(2)}, u32[]{:S(2)}) collective-permute-start(bf16[1,64,2048]{2,1,0:T(8,128)(2,1)S(1)} %get-tuple-element.136), channel_id=1, source_target_pairs={{0,2},{1,3},{2,0},{3,1},{4,6},{5,7},{6,4},{7,5},{8,10},{9,11},{10,... | collective-permute-start | bytes 786440 | tf_op jit(solution)/shard_map/ppermute | solution.py:289
  67.7 7.0 %collective-permute-start.46 = (bf16[1,64,2048]{2,1,0:T(8,128)(2,1)S(1)}, bf16[1,64,2048]{2,1,0:T(8,128)(2,1)S(1)}, u32[]{:S(2)}, u32[]{:S(2)}) collective-permute-start(bf16[1,64,2048]{2,1,0:T(8,128)(2,1)S(1)} %get-tuple-element.137), channel_id=1, source_target_pairs={{0,4},{1,5},{2,6},{3,7},{4,0},{5,1},{6,2},{7,3},{8,12},{9,13},{10,... | collective-permute-start | bytes 786440 | tf_op jit(solution)/shard_map/ppermute | solution.py:289
  73.3 14.5 %copy-start.1 = (bf16[2,64,2048]{2,1,0:T(8,128)(2,1)}, bf16[2,64,2048]{2,1,0:T(8,128)(2,1)S(1)}, u32[]{:S(2)}) copy-start(bf16[2,64,2048]{2,1,0:T(8,128)(2,1)S(1)} %pad_maximum_fusion.5) | copy-start | bytes 1572868
  74.7 11.9 %collective-permute-start.48 = (bf16[2,64,2048]{2,1,0:T(8,128)(2,1)S(1)}, bf16[2,64,2048]{2,1,0:T(8,128)(2,1)}, u32[]{:S(2)}, u32[]{:S(2)}) collective-permute-start(bf16[2,64,2048]{2,1,0:T(8,128)(2,1)S(1)} %pad_maximum_fusion.4), channel_id=1, source_target_pairs={{0,2},{1,3},{2,0},{3,1},{4,6},{5,7},{6,4},{7,5},{8,10},{9,11},{10,... | collective-permute-start | bytes 1572872 | tf_op jit(solution)/shard_map/ppermute | solution.py:289
  75.2 12.6 %collective-permute-start.49 = (bf16[2,64,2048]{2,1,0:T(8,128)(2,1)S(1)}, bf16[2,64,2048]{2,1,0:T(8,128)(2,1)S(1)}, u32[]{:S(2)}, u32[]{:S(2)}) collective-permute-start(bf16[2,64,2048]{2,1,0:T(8,128)(2,1)S(1)} %pad_maximum_fusion.5), channel_id=1, source_target_pairs={{0,4},{1,5},{2,6},{3,7},{4,0},{5,1},{6,2},{7,3},{8,12},{9,13},{10,... | collective-permute-start | bytes 1572872 | tf_op jit(solution)/shard_map/ppermute | solution.py:289
  90.4 4.5 %collective-permute-start.50 = (bf16[2,4,64,2048]{3,2,1,0:T(8,128)(2,1)}, bf16[2,4,64,2048]{3,2,1,0:T(8,128)(2,1)}, u32[]{:S(2)}, u32[]{:S(2)}) collective-permute-start(bf16[2,4,64,2048]{3,2,1,0:T(8,128)(2,1)} %pad_maximum_fusion.1), channel_id=1, source_target_pairs={{0,1},{1,0},{2,3},{3,2},{4,5},{5,4},{6,7},{7,6},{8,9},{9,8},{10,11... | collective-permute-start | bytes 6291464 | tf_op jit(solution)/shard_map/ppermute | solution.py:289
  92.3 4.4 %copy-start.7 = (bf16[2,2048,512]{2,1,0:T(8,128)(2,1)S(1)}, bf16[2,2048,512]{2,1,0:T(8,128)(2,1)}, u32[]{:S(2)}) copy-start(bf16[2,2048,512]{2,1,0:T(8,128)(2,1)} %param.81) | copy-start | bytes 12582916
  99.0 2.3 %copy-start.8 = (bf16[2,2048,512]{2,1,0:T(8,128)(2,1)S(1)}, bf16[2,2048,512]{2,1,0:T(8,128)(2,1)}, u32[]{:S(2)}) copy-start(bf16[2,2048,512]{2,1,0:T(8,128)(2,1)} %param.82) | copy-start | bytes 12582916
  104.0 2.6 %copy-start.9 = (bf16[2,512,2048]{2,1,0:T(8,128)(2,1)S(1)}, bf16[2,512,2048]{2,1,0:T(8,128)(2,1)}, u32[]{:S(2)}) copy-start(bf16[2,512,2048]{2,1,0:T(8,128)(2,1)} %param.83) | copy-start | bytes 12582916
  111.7 4.2 %collective-permute-start.51 = (bf16[2,4,64,2048]{3,2,1,0:T(8,128)(2,1)S(1)}, bf16[2,4,64,2048]{3,2,1,0:T(8,128)(2,1)S(1)}, u32[]{:S(2)}, u32[]{:S(2)}) collective-permute-start(bf16[2,4,64,2048]{3,2,1,0:T(8,128)(2,1)S(1)} %bitcast.116), channel_id=1, source_target_pairs={{0,1},{1,0},{2,3},{3,2},{4,5},{5,4},{6,7},{7,6},{8,9},{9,8},{10,11... | collective-permute-start | bytes 6291464 | tf_op jit(solution)/shard_map/ppermute | solution.py:289
  116.9 14.0 %collective-permute-start.53 = (bf16[2,64,2048]{2,1,0:T(8,128)(2,1)S(1)}, bf16[2,64,2048]{2,1,0:T(8,128)(2,1)S(1)}, u32[]{:S(2)}, u32[]{:S(2)}) collective-permute-start(bf16[2,64,2048]{2,1,0:T(8,128)(2,1)S(1)} %slice.240), channel_id=1, source_target_pairs={{0,4},{1,5},{2,6},{3,7},{4,0},{5,1},{6,2},{7,3},{8,12},{9,13},{10,... | collective-permute-start | bytes 1572872 | tf_op jit(solution)/shard_map/ppermute | solution.py:289
  117.1 13.9 %collective-permute-start.52 = (bf16[2,64,2048]{2,1,0:T(8,128)(2,1)S(1)}, bf16[2,64,2048]{2,1,0:T(8,128)(2,1)S(1)}, u32[]{:S(2)}, u32[]{:S(2)}) collective-permute-start(bf16[2,64,2048]{2,1,0:T(8,128)(2,1)S(1)} %slice.241), channel_id=1, source_target_pairs={{0,2},{1,3},{2,0},{3,1},{4,6},{5,7},{6,4},{7,5},{8,10},{9,11},{10,... | collective-permute-start | bytes 1572872 | tf_op jit(solution)/shard_map/ppermute | solution.py:289
  131.2 7.6 %collective-permute-start.55 = (bf16[1,64,2048]{2,1,0:T(8,128)(2,1)S(1)}, bf16[1,64,2048]{2,1,0:T(8,128)(2,1)S(1)}, u32[]{:S(2)}, u32[]{:S(2)}) collective-permute-start(bf16[1,64,2048]{2,1,0:T(8,128)(2,1)S(1)} %slice.242), channel_id=1, source_target_pairs={{0,2},{1,3},{2,0},{3,1},{4,6},{5,7},{6,4},{7,5},{8,10},{9,11},{10,... | collective-permute-start | bytes 786440 | tf_op jit(solution)/shard_map/ppermute | solution.py:289
  132.0 7.3 %collective-permute-start.54 = (bf16[1,64,2048]{2,1,0:T(8,128)(2,1)S(1)}, bf16[1,64,2048]{2,1,0:T(8,128)(2,1)S(1)}, u32[]{:S(2)}, u32[]{:S(2)}) collective-permute-start(bf16[1,64,2048]{2,1,0:T(8,128)(2,1)S(1)} %slice.243), channel_id=1, source_target_pairs={{0,4},{1,5},{2,6},{3,7},{4,0},{5,1},{6,2},{7,3},{8,12},{9,13},{10,... | collective-permute-start | bytes 786440 | tf_op jit(solution)/shard_map/ppermute | solution.py:289
